TPU v7x, 128 devices: a whole 4x4x4 slice. The times are simulated.
128 devices in a mesh: sky: 8 (over x, y_hi), epoch: 16 (over y_lo, z, core).
Axes of the slice: x: 4, y: 4 (y_hi: 2, y_lo: 2; y = y_hi * 2 + y_lo), z: 4, core: 2. Of those that a mesh axis runs over, the one named last changes fastest.
Arguments:
- psi: bfloat16 [16, 512, 4096], P('epoch', 'sky'), may hold values from -6 to 6
- phi: bfloat16 [16, 512, 4096], P('epoch', 'sky'), may hold values from 0.25 to 4
- row_shift: int32 [16, 64], P(None, 'epoch'), may hold values from -8 to 8, as said below
- col_shift: int32 [16, 64], P(None, 'epoch'), may hold values from -64 to 64, as said below
Outputs:
- psi_stack: float32 [64, 512, 4096], P('epoch', 'sky')
- phi_stack: float32 [64, 512, 4096], P('epoch', 'sky')
Inputs may be any that keep to these rules, and one draw needn't show every extreme that they name: `row_shift`: both ends of the range are taken by some epoch and hypothesis. `col_shift`: both ends of the range are taken by some epoch and hypothesis.
All inputs are finite; a program needn't handle non-finite values.
Results may differ from a plain program's by a relative error of at most 0.0003.
Values may be sent and summed in bfloat16 or wider, within the bound.
No kernel may reach another device: no remote copies, remote signals or barrier semaphores. Data moves between devices by JAX's collectives and lax.ppermute only.
A program may use at most 192 MiB of HBM per device.

v0:
```python
import jax
import jax.numpy as jnp
from jax import lax
from jax.sharding import PartitionSpec as P

DEPTH = 8
XMAX = 64


def with_halo(cells, sides, width):
    for axis, dim in sides:
        count = lax.axis_size(axis)
        ends = count - 1
        head = lax.slice_in_dim(cells, 0, width, axis=dim)
        tail = lax.slice_in_dim(cells, cells.shape[dim] - width, cells.shape[dim], axis=dim)
        cells = jnp.concatenate(
            [
                lax.ppermute(tail, axis, [(i, (i + 1) % count) for i in range(ends)]),
                cells,
                lax.ppermute(head, axis, [((i + 1) % count, i) for i in range(ends)]),
            ],
            axis=dim,
        )
    return cells


def make_folder(row_shift, col_shift, row_pad, out_rows, col_count):

    def fold_epochs(running, received, first_index):
        epoch_count = received.shape[0]
        padded = jnp.pad(received, ((0, 0), (0, 0), (row_pad, row_pad), (XMAX, XMAX)))
        epoch_ids = jnp.arange(epoch_count, dtype=jnp.int32)

        def shift_cut(epoch_id, row_off, col_off):
            window = lax.dynamic_slice(
                padded,
                (epoch_id, jnp.int32(0), DEPTH + row_off, XMAX + col_off),
                (1, 2, out_rows, col_count),
            )
            return window[0]

        def one_hypothesis(hyp_index, totals):
            row_offsets = lax.dynamic_index_in_dim(row_shift, hyp_index, 1, keepdims=False)
            col_offsets = lax.dynamic_index_in_dim(col_shift, hyp_index, 1, keepdims=False)
            windows = jax.vmap(shift_cut)(epoch_ids, row_offsets, col_offsets)
            before = lax.dynamic_index_in_dim(totals, hyp_index, 0, keepdims=False)
            after = before + jnp.sum(windows.astype(jnp.float32), axis=0)
            return lax.dynamic_update_index_in_dim(totals, after, hyp_index, 0)

        return lax.fori_loop(0, running.shape[0], one_hypothesis, running)

    return fold_epochs


def body(psi, phi, row_shift, col_shift):
    row_count = psi.shape[1]
    col_count = psi.shape[2]
    hyp_count = row_shift.shape[1]
    images = jnp.stack([psi, phi], 1)
    extended = with_halo(images, (("sky", 2),), DEPTH)
    folder = make_folder(row_shift, col_shift, 0, row_count, col_count)
    initial = jnp.zeros((hyp_count, 2, row_count, col_count), jnp.float32)
    stacked = folder(initial, lax.all_gather(extended, "epoch", axis=0, tiled=True), jnp.int32(0))
    return (stacked[:, 0], stacked[:, 1])


def solution(mesh):
    return jax.shard_map(
        body,
        mesh=mesh,
        in_specs=(
            P("epoch", "sky", None),
            P("epoch", "sky", None),
            P(None, "epoch"),
            P(None, "epoch"),
        ),
        out_specs=(P("epoch", "sky", None), P("epoch", "sky", None)),
        check_vma=False,
    )
```

profile of v0, /device:TPU:1, one launch (start us, length us, event | category | flops | bytes accessed | tf_op | source)
XLA Modules:
  0.0 565.2 jit_solution(6434789305987517854)
XLA Ops:
  8.2 5.7 %collective-permute-start = (bf16[1,2,8,4096]{3,2,1,0:T(8,128)(2,1)S(1)}, bf16[1,2,8,4096]{3,2,1,0:T(8,128)(2,1)S(1)}, u32[]{:S(2)}, u32[]{:S(2)}) collective-permute-start(bf16[1,2,8,4096]{3,2,1,0:T(8,128)(2,1)S(1)} %get-tuple-element.204), channel_id=1, source_target_pairs={{0,16},{16,32},{32,48},{48,64},{64,80},{80,96},{96,112},{1,17},{17... | collective-permute-start | bytes 393224 | tf_op jit(solution)/shard_map/ppermute | solution.py:18
  16.0 5.1 collective-permute-done.1
  23.4 115.2 %all-gather.2.cloned.1.call-done = bf16[16,2,80,4096]{3,2,1,0:T(8,128)(2,1)} async-done(((bf16[1,2,80,4096]{3,2,1,0:T(8,128)(2,1)}), bf16[16,2,80,4096]{3,2,1,0:T(8,128)(2,1)}) %all-gather.2.cloned.1.call-update) | async-done | bytes 20971536 | tf_op jit(solution)/shard_map/all_gather | solution.py:63
  138.6 20.3 %pad.4 = bf16[16,2,80,4224]{3,2,1,0:T(8,128)(2,1)} pad(bf16[16,2,80,4096]{3,2,1,0:T(8,128)(2,1)} %all-gather.2.cloned.1.call-done, bf16[]{:T(256)} %constant.107.clone.1), padding=0_0x0_0x0_0x64_64 | pad | bytes 42598400 | tf_op jit(solution)/shard_map/jit(_pad)/pad | solution.py:31
  163.2 387.3 %while.20 = (s32[]{:T(128)}, f32[4,2,64,4096]{3,2,0,1:T(8,128)}, s32[16,4]{0,1:T(4,128)}, s32[16,4]{0,1:T(4,128)}, bf16[16,2,80,4224]{3,2,1,0:T(8,128)(2,1)}, /*index=5*/s32[]{:T(128)}, s32[]{:T(128)}, s32[]{:T(128)}) while((s32[]{:T(128)}, f32[4,2,64,4096]{3,2,0,1:T(8,128)}, s32[16,4]{0,1:T(4,128)}, s32[16,4]{0,1:T(4,128)}, ...), condition=%wide.region_2.3_spmd.clone, body=%wide.region_0.2_spmd.clone.sunk | while | flops 16777540 | bytes 31461000 | solution.py:50
  164.0 85.8 %while.21 = (s32[]{:T(128)}, bf16[16,2,80,4224]{3,2,1,0:T(8,128)(2,1)}, s32[16,4]{0,1:T(4,128)S(1)}, bf16[16,1,2,64,4096]{4,3,2,1,0:T(8,128)(2,1)}, s32[]{:T(128)}) while((s32[]{:T(128)}, bf16[16,2,80,4224]{3,2,1,0:T(8,128)(2,1)}, s32[16,4]{0,1:T(4,128)S(1)}, bf16[16,1,2,64,4096]{4,3,2,1,0:T(8,128)(2,1)}, s32[]{:T(128)}) %tuple.68), condition=%wide.while_cond, body=%wide.while_body.sunk | while | flops 2 | bytes 2099321 | solution.py:35
  164.7 4.7 bitcast_dynamic-update-slice_fusion.5
  180.7 4.8 bitcast_dynamic-update-slice_fusion.5
  186.2 4.7 bitcast_dynamic-update-slice_fusion.5
  196.8 4.7 bitcast_dynamic-update-slice_fusion.5
  202.2 4.7 bitcast_dynamic-update-slice_fusion.5
  218.3 4.7 bitcast_dynamic-update-slice_fusion.5
  223.7 4.7 bitcast_dynamic-update-slice_fusion.5
  239.8 4.7 bitcast_dynamic-update-slice_fusion.5
  245.1 4.7 bitcast_dynamic-update-slice_fusion.5
  249.8 6.9 %convert_reduce_fusion.2 = f32[2,64,4096]{2,1,0:T(8,128)S(1)} fusion(bf16[16,1,2,64,4096]{4,3,2,1,0:T(8,128)(2,1)} %get-tuple-element.274), kind=kLoop, calls=%fused_computation.3.clone.1 | loop fusion | flops 16252928 | bytes 18874368 | tf_op jit(solution)/shard_map/while/body/eval_jaxpr/reduce_sum | solution.py:47
  260.8 85.8 %while.21 = (s32[]{:T(128)}, bf16[16,2,80,4224]{3,2,1,0:T(8,128)(2,1)}, s32[16,4]{0,1:T(4,128)S(1)}, bf16[16,1,2,64,4096]{4,3,2,1,0:T(8,128)(2,1)}, s32[]{:T(128)}) while((s32[]{:T(128)}, bf16[16,2,80,4224]{3,2,1,0:T(8,128)(2,1)}, s32[16,4]{0,1:T(4,128)S(1)}, bf16[16,1,2,64,4096]{4,3,2,1,0:T(8,128)(2,1)}, s32[]{:T(128)}) %tuple.68), condition=%wide.while_cond, body=%wide.while_body.sunk | while | flops 2 | bytes 2099321 | solution.py:35
  261.5 4.7 bitcast_dynamic-update-slice_fusion.5
  277.6 4.8 bitcast_dynamic-update-slice_fusion.5
  283.0 4.7 bitcast_dynamic-update-slice_fusion.5
  293.7 4.7 bitcast_dynamic-update-slice_fusion.5
  299.0 4.7 bitcast_dynamic-update-slice_fusion.5
  315.2 4.7 bitcast_dynamic-update-slice_fusion.5
  336.6 4.7 bitcast_dynamic-update-slice_fusion.5
  341.9 4.7 bitcast_dynamic-update-slice_fusion.5
  346.6 6.9 %convert_reduce_fusion.2 = f32[2,64,4096]{2,1,0:T(8,128)S(1)} fusion(bf16[16,1,2,64,4096]{4,3,2,1,0:T(8,128)(2,1)} %get-tuple-element.274), kind=kLoop, calls=%fused_computation.3.clone.1 | loop fusion | flops 16252928 | bytes 18874368 | tf_op jit(solution)/shard_map/while/body/eval_jaxpr/reduce_sum | solution.py:47
  357.6 85.9 %while.21 = (s32[]{:T(128)}, bf16[16,2,80,4224]{3,2,1,0:T(8,128)(2,1)}, s32[16,4]{0,1:T(4,128)S(1)}, bf16[16,1,2,64,4096]{4,3,2,1,0:T(8,128)(2,1)}, s32[]{:T(128)}) while((s32[]{:T(128)}, bf16[16,2,80,4224]{3,2,1,0:T(8,128)(2,1)}, s32[16,4]{0,1:T(4,128)S(1)}, bf16[16,1,2,64,4096]{4,3,2,1,0:T(8,128)(2,1)}, s32[]{:T(128)}) %tuple.68), condition=%wide.while_cond, body=%wide.while_body.sunk | while | flops 2 | bytes 2099321 | solution.py:35
  358.3 4.7 bitcast_dynamic-update-slice_fusion.5
  374.3 4.8 bitcast_dynamic-update-slice_fusion.5
  379.8 4.7 bitcast_dynamic-update-slice_fusion.5
  390.5 4.7 bitcast_dynamic-update-slice_fusion.5
  395.8 4.7 bitcast_dynamic-update-slice_fusion.5
  412.0 4.7 bitcast_dynamic-update-slice_fusion.5
  417.3 4.7 bitcast_dynamic-update-slice_fusion.5
  433.4 4.7 bitcast_dynamic-update-slice_fusion.5
  438.8 4.7 bitcast_dynamic-update-slice_fusion.5
  443.5 6.9 %convert_reduce_fusion.2 = f32[2,64,4096]{2,1,0:T(8,128)S(1)} fusion(bf16[16,1,2,64,4096]{4,3,2,1,0:T(8,128)(2,1)} %get-tuple-element.274), kind=kLoop, calls=%fused_computation.3.clone.1 | loop fusion | flops 16252928 | bytes 18874368 | tf_op jit(solution)/shard_map/while/body/eval_jaxpr/reduce_sum | solution.py:47
  454.4 85.9 %while.21 = (s32[]{:T(128)}, bf16[16,2,80,4224]{3,2,1,0:T(8,128)(2,1)}, s32[16,4]{0,1:T(4,128)S(1)}, bf16[16,1,2,64,4096]{4,3,2,1,0:T(8,128)(2,1)}, s32[]{:T(128)}) while((s32[]{:T(128)}, bf16[16,2,80,4224]{3,2,1,0:T(8,128)(2,1)}, s32[16,4]{0,1:T(4,128)S(1)}, bf16[16,1,2,64,4096]{4,3,2,1,0:T(8,128)(2,1)}, s32[]{:T(128)}) %tuple.68), condition=%wide.while_cond, body=%wide.while_body.sunk | while | flops 2 | bytes 2099321 | solution.py:35
  455.1 4.7 bitcast_dynamic-update-slice_fusion.5
  471.2 4.8 bitcast_dynamic-update-slice_fusion.5
  476.6 4.7 bitcast_dynamic-update-slice_fusion.5
  487.3 4.7 bitcast_dynamic-update-slice_fusion.5
  492.7 4.7 bitcast_dynamic-update-slice_fusion.5
  508.8 4.7 bitcast_dynamic-update-slice_fusion.5
  514.2 4.7 bitcast_dynamic-update-slice_fusion.5
  530.3 4.7 bitcast_dynamic-update-slice_fusion.5
  540.3 6.9 %convert_reduce_fusion.2 = f32[2,64,4096]{2,1,0:T(8,128)S(1)} fusion(bf16[16,1,2,64,4096]{4,3,2,1,0:T(8,128)(2,1)} %get-tuple-element.274), kind=kLoop, calls=%fused_computation.3.clone.1 | loop fusion | flops 16252928 | bytes 18874368 | tf_op jit(solution)/shard_map/while/body/eval_jaxpr/reduce_sum | solution.py:47
  550.5 7.9 %slice_bitcast_fusion = (f32[4,64,4096]{2,1,0:T(8,128)}, f32[4,64,4096]{2,1,0:T(8,128)}) fusion(f32[4,2,64,4096]{3,2,0,1:T(8,128)} %get-tuple-element.157), kind=kLoop, calls=%fused_computation.12 | loop fusion | bytes 16777216 | tf_op jit(solution)/shard_map/squeeze | solution.py:64
  (193 shorter events, 209.0 us)
Async XLA Ops:
  7.2 131.5 %all-gather.2.cloned.1.call-start = ((), (), s32[]{:S(2)}) async-start(), calls=%async_computation | async-start | bytes 22282240 | tf_op jit(solution)/shard_map/all_gather | solution.py:63
  8.2 7.8 %collective-permute-start = (bf16[1,2,8,4096]{3,2,1,0:T(8,128)(2,1)S(1)}, bf16[1,2,8,4096]{3,2,1,0:T(8,128)(2,1)S(1)}, u32[]{:S(2)}, u32[]{:S(2)}) collective-permute-start(bf16[1,2,8,4096]{3,2,1,0:T(8,128)(2,1)S(1)} %get-tuple-element.204), channel_id=1, source_target_pairs={{0,16},{16,32},{32,48},{48,64},{64,80},{80,96},{96,112},{1,17},{17... | collective-permute-start | bytes 393224 | tf_op jit(solution)/shard_map/ppermute | solution.py:18
  13.8 7.2 %collective-permute-start.1 = (bf16[1,2,8,4096]{3,2,1,0:T(8,128)(2,1)S(1)}, bf16[1,2,8,4096]{3,2,1,0:T(8,128)(2,1)S(1)}, u32[]{:S(2)}, u32[]{:S(2)}) collective-permute-start(bf16[1,2,8,4096]{3,2,1,0:T(8,128)(2,1)S(1)} %get-tuple-element.205), channel_id=1, source_target_pairs={{16,0},{32,16},{48,32},{64,48},{80,64},{96,80},{112,96},{17,1},{33... | collective-permute-start | bytes 393224 | tf_op jit(solution)/shard_map/ppermute | solution.py:20
Sparse Core Ops, SparseCore 0:
  23.6 115.0 all-gather.1
where the time goes:
time: 570 us; the launch traced here: 565 us
  local copies, waits for them, and re-layouts  383 us (67%)
  waiting for transfers between devices  121 us (21%)
  other arithmetic  40 us (7%)
  between operations  14 us (2%)
  starting transfers between devices  6.98 us (1%)
    gather x192, local copies, waits for them, and re-layouts  343 us
    all_gather x1, waiting for transfers between devices, body(): lax.all_gather(extended, 'epoch', axis=0, tiled=True)  115 us
    reduce_sum x4, other arithmetic, one_hypothesis(): after = before + jnp.sum(windows.astype(jnp.float32), axis=0)  27.6 us
    pad x1, local copies, waits for them, and re-layouts, fold_epochs(): jnp.pad(received, ((0, 0), (0, 0), (row_pad, row_pad), (XMAX, XMAX)))  20.3 us
  transfers between devices with their start and end apart: 3, of which 3 were waited for; matrix products, arithmetic and copies ran while one was open for 0% of the time, Pallas kernels for 0%

commit v1 on v0

v1 whole, which is shorter than its diff:
```python
import functools

import jax
import jax.numpy as jnp
from jax import lax
from jax.experimental import pallas as pl
from jax.experimental.pallas import tpu as pltpu
from jax.sharding import PartitionSpec as P

DEPTH = 8
XMAX = 64
LANES = 128
BLOCK_COLS = 512
CHUNK_ROWS = 32


def with_halo(cells, sides, width):
    for axis, dim in sides:
        count = lax.axis_size(axis)
        ends = count - 1
        head = lax.slice_in_dim(cells, 0, width, axis=dim)
        tail = lax.slice_in_dim(cells, cells.shape[dim] - width, cells.shape[dim], axis=dim)
        cells = jnp.concatenate(
            [
                lax.ppermute(tail, axis, [(i, (i + 1) % count) for i in range(ends)]),
                cells,
                lax.ppermute(head, axis, [((i + 1) % count, i) for i in range(ends)]),
            ],
            axis=dim,
        )
    return cells


def stack_kernel(rs_ref, cs_ref, mid_ref, left_ref, right_ref, psi_ref, phi_ref, slab_ref,
                 *, epochs, hyps, rows_in, rows_out, width, blocks):
    j = pl.program_id(0)
    pieces = width // LANES
    slab_rows = slab_ref.shape[1]
    has_left = j > 0
    has_right = j < blocks - 1
    row_vregs = CHUNK_ROWS // 8

    for img, out_ref in ((0, psi_ref), (1, phi_ref)):
        def convert(e, carry):
            slab_ref[e, 0:rows_in, LANES:LANES + width] = mid_ref[e, img].astype(jnp.float32)
            left = left_ref[e, img].astype(jnp.float32)
            slab_ref[e, 0:rows_in, 0:LANES] = jnp.where(has_left, left, 0.0)
            right = right_ref[e, img].astype(jnp.float32)
            slab_ref[e, 0:rows_in, LANES + width:2 * LANES + width] = jnp.where(has_right, right, 0.0)
            slab_ref[e, rows_in:slab_rows, :] = jnp.zeros((slab_rows - rows_in, width + 2 * LANES), jnp.float32)
            return carry

        lax.fori_loop(0, epochs, convert, 0)

        for h in range(hyps):
            for chunk in range(rows_out // CHUNK_ROWS):
                y0 = chunk * CHUNK_ROWS

                def add_epoch(e, acc):
                    start = DEPTH + rs_ref[e * hyps + h]
                    col = cs_ref[e * hyps + h]
                    a8 = start // 8
                    b8 = start - a8 * 8
                    q = (col + LANES) // LANES - 1
                    rem = col - q * LANES
                    row0 = pl.multiple_of(y0 + a8 * 8, 8)
                    lane0 = pl.multiple_of((q + 1) * LANES, LANES)
                    sub_mask = lax.broadcasted_iota(jnp.int32, (8, LANES), 0) >= b8
                    lane_mask = lax.broadcasted_iota(jnp.int32, (8, LANES), 1) >= rem
                    sub_shift = lax.rem(8 - b8, 8)
                    lane_shift = lax.rem(LANES - rem, LANES)
                    window = slab_ref.at[e, pl.ds(row0, CHUNK_ROWS + 8), pl.ds(lane0, width + LANES)]
                    tiles = [
                        [window[8 * k:8 * k + 8, LANES * p:LANES * p + LANES] for p in range(pieces + 1)]
                        for k in range(row_vregs + 1)
                    ]
                    out = []
                    for k in range(row_vregs):
                        shifted = [
                            pltpu.roll(jnp.where(sub_mask, tiles[k][p], tiles[k + 1][p]), sub_shift, 0)
                            for p in range(pieces + 1)
                        ]
                        out.append([
                            acc[k][p] + pltpu.roll(jnp.where(lane_mask, shifted[p], shifted[p + 1]), lane_shift, 1)
                            for p in range(pieces)
                        ])
                    return out

                zero = [[jnp.zeros((8, LANES), jnp.float32) for _ in range(pieces)] for _ in range(row_vregs)]
                acc = lax.fori_loop(0, epochs, add_epoch, zero, unroll=4)
                for k in range(row_vregs):
                    for p in range(pieces):
                        out_ref[h, pl.ds(y0 + 8 * k, 8), pl.ds(LANES * p, LANES)] = acc[k][p]


def stack_call(extended, rs, cs, hyps, rows_out):
    epochs, images, rows_in, cols = extended.shape
    width = BLOCK_COLS
    blocks = cols // width
    pieces = width // LANES
    last_piece = cols // LANES - 1
    kernel = functools.partial(
        stack_kernel, epochs=epochs, hyps=hyps, rows_in=rows_in, rows_out=rows_out, width=width, blocks=blocks
    )
    grid_spec = pltpu.PrefetchScalarGridSpec(
        num_scalar_prefetch=2,
        grid=(blocks,),
        in_specs=[
            pl.BlockSpec((epochs, images, rows_in, width), lambda j, rs, cs: (0, 0, 0, j)),
            pl.BlockSpec((epochs, images, rows_in, LANES),
                         lambda j, rs, cs: (0, 0, 0, jnp.maximum(j * pieces - 1, 0))),
            pl.BlockSpec((epochs, images, rows_in, LANES),
                         lambda j, rs, cs: (0, 0, 0, jnp.minimum((j + 1) * pieces, last_piece))),
        ],
        out_specs=[
            pl.BlockSpec((hyps, rows_out, width), lambda j, rs, cs: (0, 0, j)),
            pl.BlockSpec((hyps, rows_out, width), lambda j, rs, cs: (0, 0, j)),
        ],
        scratch_shapes=[pltpu.VMEM((epochs, rows_in + 8, width + 2 * LANES), jnp.float32)],
    )
    out_shape = [jax.ShapeDtypeStruct((hyps, rows_out, cols), jnp.float32)] * 2
    flops = 2 * epochs * hyps * images * rows_out * cols
    return pl.pallas_call(
        kernel,
        grid_spec=grid_spec,
        out_shape=out_shape,
        compiler_params=pltpu.CompilerParams(dimension_semantics=("arbitrary",)),
        cost_estimate=pl.CostEstimate(
            flops=flops, transcendentals=0, bytes_accessed=extended.size * 2 + 2 * hyps * rows_out * cols * 4
        ),
        name="shift_stack",
    )(rs, cs, extended, extended, extended)


def body(psi, phi, row_shift, col_shift):
    row_count = psi.shape[1]
    hyp_count = row_shift.shape[1]
    images = jnp.stack([psi, phi], 1)
    extended = with_halo(images, (("sky", 2),), DEPTH)
    gathered = lax.all_gather(extended, "epoch", axis=0, tiled=True)
    rs = row_shift.reshape(-1)
    cs = col_shift.reshape(-1)
    psi_out, phi_out = stack_call(gathered, rs, cs, hyp_count, row_count)
    return psi_out, phi_out


def solution(mesh):
    return jax.shard_map(
        body,
        mesh=mesh,
        in_specs=(
            P("epoch", "sky", None),
            P("epoch", "sky", None),
            P(None, "epoch"),
            P(None, "epoch"),
        ),
        out_specs=(P("epoch", "sky", None), P("epoch", "sky", None)),
        check_vma=False,
    )
```

time: 570 us -> 234 us (0.41)
  local copies, waits for them, and re-layouts: 383 us -> 1.45 us
  Pallas kernels: 0 us -> 88.2 us
  other arithmetic: 40 us -> 3.33 us
    gather x192 -> x0, local copies, waits for them, and re-layouts: 343 us -> none
    pallas_call x0 -> x1, Pallas kernels: none -> 88.2 us  [stack_call(): pl.pallas_call(kernel, grid_spec=grid_spec, out_shape=out_shape, compiler...]
    reduce_sum x4 -> x0, other arithmetic: 27.6 us -> none  [one_hypothesis(): after = before + jnp.sum(windows.astype(jnp.float32), axis=0)]
    pad x1 -> x0, local copies, waits for them, and re-layouts: 20.3 us -> none  [fold_epochs(): jnp.pad(received, ((0, 0), (0, 0), (row_pad, row_pad), (XMAX, XMAX)))]
    squeeze x1 -> x0, local copies, waits for them, and re-layouts: 7.85 us -> none  [body(): return (stacked[:, 0], stacked[:, 1])]
    dynamic_slice x4 -> x0, local copies, waits for them, and re-layouts: 7.02 us -> none  [one_hypothesis(): before = lax.dynamic_index_in_dim(totals, hyp_index, 0, keepdims=False)]
    dynamic_update_slice x4 -> x0, other arithmetic: 6.25 us -> none  [one_hypothesis(): return lax.dynamic_update_index_in_dim(totals, after, hyp_index, 0)]
  transfers between devices with their start and end apart: 3 -> 3, of which waited for: 3 -> 3; matrix products, arithmetic and copies ran while one was open for 0% -> 1% of each run, Pallas kernels for 0% -> 0%
where the time goes in v1:
time: 234 us
  waiting for transfers between devices  120 us (51%)
  Pallas kernels  88.2 us (38%)
  between operations  14.1 us (6%)
  starting transfers between devices  6.98 us (3%)
  other arithmetic  3.33 us (1%)
    all_gather x1, waiting for transfers between devices, body(): gathered = lax.all_gather(extended, 'epoch', axis=0, tiled=True)  114 us
    pallas_call x1, Pallas kernels, stack_call(): pl.pallas_call(kernel, grid_spec=grid_spec, out_shape=out_shape, compiler...  88.2 us
    ppermute x1, starting transfers between devices, with_halo(): lax.ppermute(tail, axis, [(i, (i + 1) % count) for i in range(ends)])  5.66 us
    ppermute x1, waiting for transfers between devices, with_halo(): lax.ppermute(head, axis, [((i + 1) % count, i) for i in range(ends)])  5.08 us
  transfers between devices with their start and end apart: 3, of which 3 were waited for; matrix products, arithmetic and copies ran while one was open for 1% of the time, Pallas kernels for 0%

profile of v1, /device:TPU:1, one launch (start us, length us, event | category | flops | bytes accessed | tf_op | source)
XLA Modules:
  0.0 233.7 jit_solution(5666724902756389976)
XLA Ops:
  7.2 0.0 all-gather.2.cloned.1.call-start
  7.2 0.0 copy-start
  7.2 0.0 copy-start.1
  7.2 1.0 pad_maximum_fusion.2
  8.2 5.7 %collective-permute-start = (bf16[1,2,8,4096]{3,2,1,0:T(8,128)(2,1)S(1)}, bf16[1,2,8,4096]{3,2,1,0:T(8,128)(2,1)S(1)}, u32[]{:S(2)}, u32[]{:S(2)}) collective-permute-start(bf16[1,2,8,4096]{3,2,1,0:T(8,128)(2,1)S(1)} %get-tuple-element.2), channel_id=1, source_target_pairs={{0,16},{16,32},{32,48},{48,64},{64,80},{80,96},{96,112},{1,17},{17... | collective-permute-start | bytes 393224 | tf_op jit(solution)/shard_map/ppermute | solution.py:25
  13.9 1.3 collective-permute-start.1
  15.2 0.8 collective-permute-done
  16.0 5.1 %collective-permute-done.1 = bf16[1,2,8,4096]{3,2,1,0:T(8,128)(2,1)S(1)} collective-permute-done((bf16[1,2,8,4096]{3,2,1,0:T(8,128)(2,1)S(1)}, bf16[1,2,8,4096]{3,2,1,0:T(8,128)(2,1)S(1)}, u32[]{:S(2)}, u32[]{:S(2)}) %collective-permute-start.1) | collective-permute-done | bytes 131104 | tf_op jit(solution)/shard_map/ppermute | solution.py:27
  21.1 2.4 %pad_maximum_fusion = bf16[1,2,80,4096]{3,2,1,0:T(8,128)(2,1)} fusion(bf16[1,2,8,4096]{3,2,1,0:T(8,128)(2,1)S(1)} %collective-permute-done.1, bf16[1,1,64,4096]{3,2,1,0:T(8,128)(2,1)} %bitcast.3, bf16[1,1,64,4096]{3,2,1,0:T(8,128)(2,1)} %bitcast.5, bf16[1,2,8,4096]{3,2,1,0:T(8,128)(2,1)S(1)} %collective-permute-done), kind=kLoop, calls=%fused_computation | loop fusion | flops 5242880 | bytes 2621440 | tf_op jit(solution)/shard_map/concatenate | solution.py:23
  23.4 0.0 all-gather.2.cloned.1.call-update
  23.5 0.0 copy-done
  23.5 0.1 copy.10
  23.6 0.6 reshape.10.rs_ref
  24.2 0.0 copy-done.1
  24.2 0.1 copy.11
  24.3 0.7 reshape.11.cs_ref
  24.9 113.7 %all-gather.2.cloned.1.call-done.mid_ref.left_ref.right_ref = bf16[16,2,80,4096]{3,2,1,0:T(8,128)(2,1)} async-done(((bf16[1,2,80,4096]{3,2,1,0:T(8,128)(2,1)}), bf16[16,2,80,4096]{3,2,1,0:T(8,128)(2,1)}) %all-gather.2.cloned.1.call-update) | async-done | bytes 20971536 | tf_op jit(solution)/shard_map/all_gather | solution.py:140
  138.7 88.2 %shift_stack.1 = (f32[4,64,4096]{2,1,0:T(8,128)}, f32[4,64,4096]{2,1,0:T(8,128)}) custom-call(s32[64]{0:T(128)} %reshape.10.rs_ref, s32[64]{0:T(128)} %reshape.11.cs_ref, bf16[16,2,80,4096]{3,2,1,0:T(8,128)(2,1)} %all-gather.2.cloned.1.call-done.mid_ref.left_ref.right_ref, bf16[16,2,80,4096]{3,2,1,0:T(8,128)(2,1)} %all-gather.2.cloned.1.call-done.mid_ref.left_ref.right_ref, ...), custom_call_target="tpu_custom_call" | custom-call | flops 67108864 | bytes 29360128 | tf_op jit(solution)/shard_map/shift_stack/pallas_call | solution.py:123
Async XLA Ops:
  7.2 131.5 %all-gather.2.cloned.1.call-start = ((), (), s32[]{:S(2)}) async-start(), calls=%async_computation | async-start | bytes 22282240 | tf_op jit(solution)/shard_map/all_gather | solution.py:140
  7.2 16.3 %copy-start = (s32[16,4]{0,1:T(4,128)S(1)}, s32[16,4]{0,1:T(4,128)}, u32[]{:S(2)}) copy-start(s32[16,4]{0,1:T(4,128)} %param.6) | copy-start | bytes 772
  7.2 17.0 %copy-start.1 = (s32[16,4]{0,1:T(4,128)S(1)}, s32[16,4]{0,1:T(4,128)}, u32[]{:S(2)}) copy-start(s32[16,4]{0,1:T(4,128)} %param.7) | copy-start | bytes 772
  8.2 7.8 %collective-permute-start = (bf16[1,2,8,4096]{3,2,1,0:T(8,128)(2,1)S(1)}, bf16[1,2,8,4096]{3,2,1,0:T(8,128)(2,1)S(1)}, u32[]{:S(2)}, u32[]{:S(2)}) collective-permute-start(bf16[1,2,8,4096]{3,2,1,0:T(8,128)(2,1)S(1)} %get-tuple-element.2), channel_id=1, source_target_pairs={{0,16},{16,32},{32,48},{48,64},{64,80},{80,96},{96,112},{1,17},{17... | collective-permute-start | bytes 393224 | tf_op jit(solution)/shard_map/ppermute | solution.py:25
  13.9 7.2 %collective-permute-start.1 = (bf16[1,2,8,4096]{3,2,1,0:T(8,128)(2,1)S(1)}, bf16[1,2,8,4096]{3,2,1,0:T(8,128)(2,1)S(1)}, u32[]{:S(2)}, u32[]{:S(2)}) collective-permute-start(bf16[1,2,8,4096]{3,2,1,0:T(8,128)(2,1)S(1)} %get-tuple-element.3), channel_id=1, source_target_pairs={{16,0},{32,16},{48,32},{64,48},{80,64},{96,80},{112,96},{17,1},{33... | collective-permute-start | bytes 393224 | tf_op jit(solution)/shard_map/ppermute | solution.py:27
Sparse Core Ops, SparseCore 0:
  23.6 115.0 all-gather.1

commit v2 on v0

v2 whole, which is shorter than its diff:
```python
import functools

import jax
import jax.numpy as jnp
from jax import lax
from jax.experimental import pallas as pl
from jax.experimental.pallas import tpu as pltpu
from jax.sharding import PartitionSpec as P

DEPTH = 8
XMAX = 64
LANES = 128
BLOCK_COLS = 512
CHUNK_ROWS = 32
GATHER_COLS = 1024
COST_SCALE = 1000
LOOKAHEAD = 2


def with_halo(cells, sides, width):
    for axis, dim in sides:
        count = lax.axis_size(axis)
        ends = count - 1
        head = lax.slice_in_dim(cells, 0, width, axis=dim)
        tail = lax.slice_in_dim(cells, cells.shape[dim] - width, cells.shape[dim], axis=dim)
        cells = jnp.concatenate(
            [
                lax.ppermute(tail, axis, [(i, (i + 1) % count) for i in range(ends)]),
                cells,
                lax.ppermute(head, axis, [((i + 1) % count, i) for i in range(ends)]),
            ],
            axis=dim,
        )
    return cells


def chunk_kernel(rs_ref, cs_ref, mid_ref, left_ref, psi_in, phi_in, psi_hbm, phi_hbm, slab_ref, out_vmem, sems,
                 *, first, last, epochs, hyps, rows_in, rows_out, chunk, out_lo, out_hi, col_base):
    del psi_in, phi_in
    side = left_ref.shape[-1]
    slab_rows = slab_ref.shape[1]
    slab_cols = slab_ref.shape[2]
    row_vregs = CHUNK_ROWS // 8
    width = out_hi - out_lo
    subs = []
    at = out_lo
    while at < out_hi:
        pieces = min(BLOCK_COLS // LANES, (out_hi - at) // LANES)
        subs.append((at, pieces))
        at += pieces * LANES
    copies = []
    for img, out_hbm in ((0, psi_hbm), (1, phi_hbm)):
        def convert(e, carry):
            if first:
                slab_ref[e, 0:rows_in, 0:side] = jnp.zeros((rows_in, side), jnp.float32)
            else:
                slab_ref[e, 0:rows_in, 0:side] = left_ref[e, img].astype(jnp.float32)
            slab_ref[e, 0:rows_in, side:side + chunk] = mid_ref[e, img].astype(jnp.float32)
            slab_ref[e, 0:rows_in, side + chunk:slab_cols] = jnp.zeros((rows_in, slab_cols - side - chunk), jnp.float32)
            slab_ref[e, rows_in:slab_rows, :] = jnp.zeros((slab_rows - rows_in, slab_cols), jnp.float32)
            return carry

        lax.fori_loop(0, epochs, convert, 0)

        for h in range(hyps):
            for rchunk in range(rows_out // CHUNK_ROWS):
                y0 = rchunk * CHUNK_ROWS
                for base_o, pieces in subs:
                    def add_epoch(e, acc, base_o=base_o, pieces=pieces):
                        start = DEPTH + rs_ref[e * hyps + h]
                        col = cs_ref[e * hyps + h]
                        a8 = start // 8
                        b8 = start - a8 * 8
                        q = (col + LANES) // LANES - 1
                        rem = col - q * LANES
                        row0 = pl.multiple_of(y0 + a8 * 8, 8)
                        lane0 = pl.multiple_of(base_o + q * LANES, LANES)
                        sub_mask = lax.broadcasted_iota(jnp.int32, (8, LANES), 0) >= b8
                        lane_mask = lax.broadcasted_iota(jnp.int32, (8, LANES), 1) >= rem
                        sub_shift = lax.rem(8 - b8, 8)
                        lane_shift = lax.rem(LANES - rem, LANES)
                        window = slab_ref.at[e, pl.ds(row0, CHUNK_ROWS + 8), pl.ds(lane0, (pieces + 1) * LANES)]
                        tiles = [
                            [window[8 * k:8 * k + 8, LANES * p:LANES * p + LANES] for p in range(pieces + 1)]
                            for k in range(row_vregs + 1)
                        ]
                        out = []
                        for k in range(row_vregs):
                            shifted = [
                                pltpu.roll(jnp.where(sub_mask, tiles[k][p], tiles[k + 1][p]), sub_shift, 0)
                                for p in range(pieces + 1)
                            ]
                            out.append([
                                acc[k][p]
                                + pltpu.roll(jnp.where(lane_mask, shifted[p], shifted[p + 1]), lane_shift, 1)
                                for p in range(pieces)
                            ])
                        return out

                    zero = [[jnp.zeros((8, LANES), jnp.float32) for _ in range(pieces)] for _ in range(row_vregs)]
                    acc = lax.fori_loop(0, epochs, add_epoch, zero, unroll=4)
                    for k in range(row_vregs):
                        for p in range(pieces):
                            lo = base_o - out_lo + LANES * p
                            out_vmem[img, h, pl.ds(y0 + 8 * k, 8), pl.ds(lo, LANES)] = acc[k][p]
        copy = pltpu.make_async_copy(
            out_vmem.at[img, :, :, pl.ds(0, width)],
            out_hbm.at[:, :, pl.ds(col_base + out_lo, width)],
            sems.at[img],
        )
        copy.start()
        copies.append(copy)
    for copy in copies:
        copy.wait()


def chunk_call(mid, left, rs, cs, psi_acc, phi_acc, *, index, count, rows_out):
    epochs, images, rows_in, chunk = mid.shape
    hyps = psi_acc.shape[0]
    cols = psi_acc.shape[2]
    side = 2 * LANES
    first = index == 0
    last = index == count - 1
    out_lo = side if first else side - LANES
    out_hi = side + chunk if last else side + chunk - LANES
    col_base = index * chunk - side
    kernel = functools.partial(
        chunk_kernel, first=first, last=last, epochs=epochs, hyps=hyps, rows_in=rows_in, rows_out=rows_out,
        chunk=chunk, out_lo=out_lo, out_hi=out_hi, col_base=col_base,
    )
    width = out_hi - out_lo
    vmem = pltpu.MemorySpace.VMEM
    smem = pltpu.MemorySpace.SMEM
    flops = 2 * epochs * hyps * images * rows_out * width * COST_SCALE
    return pl.pallas_call(
        kernel,
        out_shape=[jax.ShapeDtypeStruct((hyps, rows_out, cols), jnp.float32)] * 2,
        in_specs=[
            pl.BlockSpec(memory_space=smem),
            pl.BlockSpec(memory_space=smem),
            pl.BlockSpec(memory_space=vmem),
            pl.BlockSpec(memory_space=vmem),
            pl.BlockSpec(memory_space=pl.ANY),
            pl.BlockSpec(memory_space=pl.ANY),
        ],
        out_specs=[pl.BlockSpec(memory_space=pl.ANY), pl.BlockSpec(memory_space=pl.ANY)],
        scratch_shapes=[
            pltpu.VMEM((epochs, rows_in + 8, side + chunk + LANES), jnp.float32),
            pltpu.VMEM((images, hyps, rows_out, chunk + LANES), jnp.float32),
            pltpu.SemaphoreType.DMA((2,)),
        ],
        input_output_aliases={4: 0, 5: 1},
        compiler_params=pltpu.CompilerParams(vmem_limit_bytes=60 * 1024 * 1024),
        cost_estimate=pl.CostEstimate(
            flops=flops, transcendentals=0,
            bytes_accessed=(mid.size + left.size) * 2 + 2 * hyps * rows_out * width * 4,
        ),
        name=f"shift_stack_{index}",
    )(rs, cs, mid, left, psi_acc, phi_acc)


def body(psi, phi, row_shift, col_shift):
    row_count = psi.shape[1]
    col_count = psi.shape[2]
    hyp_count = row_shift.shape[1]
    images = jnp.stack([psi, phi], 1)
    extended = with_halo(images, (("sky", 2),), DEPTH)
    count = col_count // GATHER_COLS
    pieces = [extended[..., GATHER_COLS * i:GATHER_COLS * (i + 1)] for i in range(count)]
    rs = row_shift.reshape(-1)
    cs = col_shift.reshape(-1)
    psi_acc = jnp.zeros((hyp_count, row_count, col_count), jnp.float32)
    phi_acc = jnp.zeros((hyp_count, row_count, col_count), jnp.float32)
    gathered = [lax.all_gather(pieces[i], "epoch", axis=0, tiled=True) for i in range(min(LOOKAHEAD, count))]
    for i in range(count):
        mid = gathered[i]
        left = gathered[i - 1][..., GATHER_COLS - 2 * LANES:] if i > 0 else mid[..., :2 * LANES]
        psi_acc, phi_acc = chunk_call(mid, left, rs, cs, psi_acc, phi_acc, index=i, count=count, rows_out=row_count)
        ahead = i + LOOKAHEAD
        if ahead < count:
            piece, psi_acc, phi_acc = lax.optimization_barrier((pieces[ahead], psi_acc, phi_acc))
            gathered.append(lax.all_gather(piece, "epoch", axis=0, tiled=True))
    return psi_acc, phi_acc


def solution(mesh):
    return jax.shard_map(
        body,
        mesh=mesh,
        in_specs=(
            P("epoch", "sky", None),
            P("epoch", "sky", None),
            P(None, "epoch"),
            P(None, "epoch"),
        ),
        out_specs=(P("epoch", "sky", None), P("epoch", "sky", None)),
        check_vma=False,
    )
```

time: 570 us -> 231 us (0.41)
  local copies, waits for them, and re-layouts: 383 us -> 16 us
  Pallas kernels: 0 us -> 106 us
  other arithmetic: 40 us -> 2.24 us
  waiting for transfers between devices: 121 us -> 84.5 us
    gather x192 -> x0, local copies, waits for them, and re-layouts: 343 us -> none
    pallas_call x0 -> x4, Pallas kernels: none -> 106 us  [chunk_call(): pl.pallas_call(kernel, out_shape=[jax.ShapeDtypeStruct((hyps, rows_out, c...]
    all_gather x1 -> x4, waiting for transfers between devices: 115 us -> 77.8 us  [the longest x2 49.4 us: body(): lax.all_gather(pieces[i], 'epoch', axis=0, tiled=True)]
    reduce_sum x4 -> x0, other arithmetic: 27.6 us -> none  [one_hypothesis(): after = before + jnp.sum(windows.astype(jnp.float32), axis=0)]
    pad x1 -> x0, local copies, waits for them, and re-layouts: 20.3 us -> none  [fold_epochs(): jnp.pad(received, ((0, 0), (0, 0), (row_pad, row_pad), (XMAX, XMAX)))]
    slice x0 -> x4, local copies, waits for them, and re-layouts: none -> 9.58 us  [the longest x2 4.99 us: body(): gathered[i - 1][..., GATHER_COLS - 2 * LANES:]]
    squeeze x1 -> x0, local copies, waits for them, and re-layouts: 7.85 us -> none  [body(): return (stacked[:, 0], stacked[:, 1])]
    dynamic_slice x4 -> x0, local copies, waits for them, and re-layouts: 7.02 us -> none  [one_hypothesis(): before = lax.dynamic_index_in_dim(totals, hyp_index, 0, keepdims=False)]
  transfers between devices with their start and end apart: 3 -> 6, of which waited for: 3 -> 6; matrix products, arithmetic and copies ran while one was open for 0% -> 6% of each run, Pallas kernels for 0% -> 32%
where the time goes in v2:
time: 231 us; the launch traced here: 230 us
  Pallas kernels  106 us (46%)
  waiting for transfers between devices  84.5 us (37%)
  local copies, waits for them, and re-layouts  16 us (7%)
  between operations  13.9 us (6%)
  starting transfers between devices  7.29 us (3%)
    pallas_call x4, Pallas kernels, chunk_call(): pl.pallas_call(kernel, out_shape=[jax.ShapeDtypeStruct((hyps, rows_out, c...  106 us
    all_gather x2, waiting for transfers between devices, body(): lax.all_gather(pieces[i], 'epoch', axis=0, tiled=True)  49.4 us
    all_gather x2, waiting for transfers between devices, body(): gathered.append(lax.all_gather(piece, 'epoch', axis=0, tiled=True))  28.5 us
    ppermute x1, starting transfers between devices, with_halo(): lax.ppermute(tail, axis, [(i, (i + 1) % count) for i in range(ends)])  5.66 us
    ppermute x1, waiting for transfers between devices, with_halo(): lax.ppermute(head, axis, [((i + 1) % count, i) for i in range(ends)])  5.1 us
    another operation x2, local copies, waits for them, and re-layouts  5 us
    slice x2, local copies, waits for them, and re-layouts, body(): gathered[i - 1][..., GATHER_COLS - 2 * LANES:]  4.99 us
  transfers between devices with their start and end apart: 6, of which 6 were waited for; matrix products, arithmetic and copies ran while one was open for 6% of the time, Pallas kernels for 32%

profile of v2, /device:TPU:1, one launch (start us, length us, event | category | flops | bytes accessed | tf_op | source)
XLA Modules:
  0.0 230.2 jit_solution(15442450176349614664)
XLA Ops:
  7.2 0.0 all-gather.7.cloned.1.call-start
  7.2 1.0 pad_maximum_fusion.2
  8.2 5.7 %collective-permute-start = (bf16[1,2,8,4096]{3,2,1,0:T(8,128)(2,1)S(1)}, bf16[1,2,8,4096]{3,2,1,0:T(8,128)(2,1)S(1)}, u32[]{:S(2)}, u32[]{:S(2)}) collective-permute-start(bf16[1,2,8,4096]{3,2,1,0:T(8,128)(2,1)S(1)} %get-tuple-element.32), channel_id=1, source_target_pairs={{0,16},{16,32},{32,48},{48,64},{64,80},{80,96},{96,112},{1,17},{17... | collective-permute-start | bytes 393224 | tf_op jit(solution)/shard_map/ppermute | solution.py:28
  13.8 0.0 copy-start
  13.8 0.0 copy-start.1
  13.9 1.3 collective-permute-start.1
  15.2 0.8 collective-permute-done
  16.0 5.1 %collective-permute-done.1 = bf16[1,2,8,4096]{3,2,1,0:T(8,128)(2,1)S(1)} collective-permute-done((bf16[1,2,8,4096]{3,2,1,0:T(8,128)(2,1)S(1)}, bf16[1,2,8,4096]{3,2,1,0:T(8,128)(2,1)S(1)}, u32[]{:S(2)}, u32[]{:S(2)}) %collective-permute-start.1) | collective-permute-done | bytes 131104 | tf_op jit(solution)/shard_map/ppermute | solution.py:30
  21.1 1.3 pad_maximum_fusion
  22.4 1.1 fusion.1
  23.4 0.0 all-gather.7.cloned.1.call-update
  23.5 0.0 all-gather.5.cloned.1.call-start
  23.5 0.7 all-gather.5.cloned.1.call-update
  24.2 0.0 all-gather.11.cloned.1.call-start
  24.3 0.0 copy-done
  24.3 0.1 copy.18
  24.4 0.6 reshape.10.rs_ref
  25.0 0.0 copy-done.1
  25.0 0.1 copy.19
  25.1 0.6 reshape.11.cs_ref
  25.7 41.0 %all-gather.7.cloned.1.call-done.mid_ref = bf16[16,2,80,1024]{3,2,1,0:T(8,128)(2,1)} async-done(((bf16[1,2,80,1024]{3,2,1,0:T(8,128)(2,1)}), bf16[16,2,80,1024]{3,2,1,0:T(8,128)(2,1)}) %all-gather.7.cloned.1.call-update) | async-done | bytes 5242896 | tf_op jit(solution)/shard_map/all_gather | solution.py:174
  66.7 3.5 %fusion = (bf16[16,2,80,256]{3,2,1,0:T(8,128)(2,1)}, bf16[16,2,80,256]{3,2,1,0:T(8,128)(2,1)}) fusion(bf16[16,2,80,1024]{3,2,1,0:T(8,128)(2,1)} %all-gather.7.cloned.1.call-done.mid_ref), kind=kLoop, calls=%fused_computation.3 | loop fusion | bytes 5242880 | tf_op jit(solution)/shard_map/slice | solution.py:177
  70.2 2.5 %broadcast_1_psi_in_phi_in.2.psi_in = f32[4,64,4096]{2,1,0:T(8,128)} broadcast(f32[]{:T(128)} %constant.0.clone.1), dimensions={} | broadcast | bytes 4194308 | tf_op jit(solution)/shard_map/broadcast.1.psi_in.phi_in
  72.7 2.5 %broadcast_1_psi_in_phi_in.2.clone.phi_in = f32[4,64,4096]{2,1,0:T(8,128)} broadcast(f32[]{:T(128)} %constant.0.clone.1), dimensions={} | broadcast | bytes 4194308 | tf_op jit(solution)/shard_map/broadcast.1.psi_in.phi_in
  75.2 24.2 %shift_stack_0.1 = (f32[4,64,4096]{2,1,0:T(8,128)}, f32[4,64,4096]{2,1,0:T(8,128)}) custom-call(s32[64]{0:T(128)} %reshape.10.rs_ref, s32[64]{0:T(128)} %reshape.11.cs_ref, bf16[16,2,80,1024]{3,2,1,0:T(8,128)(2,1)} %all-gather.7.cloned.1.call-done.mid_ref, ...), custom_call_target="tpu_custom_call", output_to_operand_aliasing={{0}: (4, {}), {1}: (5, {})} | custom-call | flops 14680064000 | bytes 8388608 | tf_op jit(solution)/shard_map/shift_stack_0/pallas_call | solution.py:135
  99.4 0.0 all-gather.11.cloned.1.call-update
  99.5 0.2 all-gather.9.cloned.1.call-start
  99.7 8.4 %all-gather.5.cloned.1.call-done.mid_ref = bf16[16,2,80,1024]{3,2,1,0:T(8,128)(2,1)} async-done(((bf16[1,2,80,1024]{3,2,1,0:T(8,128)(2,1)}), bf16[16,2,80,1024]{3,2,1,0:T(8,128)(2,1)}) %all-gather.5.cloned.1.call-update) | async-done | bytes 5242896 | tf_op jit(solution)/shard_map/all_gather | solution.py:174
  108.1 24.6 %shift_stack_1.1 = (f32[4,64,4096]{2,1,0:T(8,128)}, f32[4,64,4096]{2,1,0:T(8,128)}) custom-call(s32[64]{0:T(128)} %reshape.10.rs_ref, s32[64]{0:T(128)} %reshape.11.cs_ref, bf16[16,2,80,1024]{3,2,1,0:T(8,128)(2,1)} %all-gather.5.cloned.1.call-done.mid_ref, ...), custom_call_target="tpu_custom_call", output_to_operand_aliasing={{0}: (4, {}), {1}: (5, {})} | custom-call | flops 16777216000 | bytes 8650752 | tf_op jit(solution)/shard_map/shift_stack_1/pallas_call | solution.py:135
  132.7 0.0 all-gather.9.cloned.1.call-update
  132.7 2.5 %slice.47.left_ref = bf16[16,2,80,256]{3,2,1,0:T(8,128)(2,1)} slice(bf16[16,2,80,1024]{3,2,1,0:T(8,128)(2,1)} %all-gather.5.cloned.1.call-done.mid_ref), slice={[0:16], [0:2], [0:80], [768:1024]} | slice | bytes 2621440 | tf_op jit(solution)/shard_map/slice | solution.py:177
  135.2 14.2 %all-gather.11.cloned.1.call-done.mid_ref = bf16[16,2,80,1024]{3,2,1,0:T(8,128)(2,1)} async-done(((bf16[1,2,80,1024]{3,2,1,0:T(8,128)(2,1)}), bf16[16,2,80,1024]{3,2,1,0:T(8,128)(2,1)}) %all-gather.11.cloned.1.call-update) | async-done | bytes 5242896 | tf_op jit(solution)/shard_map/all_gather | solution.py:182
  149.4 2.5 %slice.46.left_ref = bf16[16,2,80,256]{3,2,1,0:T(8,128)(2,1)} slice(bf16[16,2,80,1024]{3,2,1,0:T(8,128)(2,1)} %all-gather.11.cloned.1.call-done.mid_ref), slice={[0:16], [0:2], [0:80], [768:1024]} | slice | bytes 2621440 | tf_op jit(solution)/shard_map/slice | solution.py:177
  151.9 24.6 %shift_stack_2.1 = (f32[4,64,4096]{2,1,0:T(8,128)}, f32[4,64,4096]{2,1,0:T(8,128)}) custom-call(s32[64]{0:T(128)} %reshape.10.rs_ref, s32[64]{0:T(128)} %reshape.11.cs_ref, bf16[16,2,80,1024]{3,2,1,0:T(8,128)(2,1)} %all-gather.11.cloned.1.call-done.mid_ref, bf16[16,2,80,256]{3,2,1,0:T(8,128)(2,1)} %slice.47.left_ref, ...), custom_call_target="tpu_custom_call", output_to_operand_aliasing={{0}: (4, {}), {1}: (5, {})} | custom-call | flops 16777216000 | bytes 8650752 | tf_op jit(solution)/shard_map/shift_stack_2/pallas_call | solution.py:135
  176.6 14.3 %all-gather.9.cloned.1.call-done.mid_ref = bf16[16,2,80,1024]{3,2,1,0:T(8,128)(2,1)} async-done(((bf16[1,2,80,1024]{3,2,1,0:T(8,128)(2,1)}), bf16[16,2,80,1024]{3,2,1,0:T(8,128)(2,1)}) %all-gather.9.cloned.1.call-update) | async-done | bytes 5242896 | tf_op jit(solution)/shard_map/all_gather | solution.py:182
  190.8 32.8 %shift_stack_3.1 = (f32[4,64,4096]{2,1,0:T(8,128)}, f32[4,64,4096]{2,1,0:T(8,128)}) custom-call(s32[64]{0:T(128)} %reshape.10.rs_ref, s32[64]{0:T(128)} %reshape.11.cs_ref, bf16[16,2,80,1024]{3,2,1,0:T(8,128)(2,1)} %all-gather.9.cloned.1.call-done.mid_ref, bf16[16,2,80,256]{3,2,1,0:T(8,128)(2,1)} %slice.46.left_ref, ...), custom_call_target="tpu_custom_call", output_to_operand_aliasing={{0}: (4, {}), {1}: (5, {})} | custom-call | flops 18874368000 | bytes 8912896 | tf_op jit(solution)/shard_map/shift_stack_3/pallas_call | solution.py:135
Async XLA Ops:
  7.2 59.5 %all-gather.7.cloned.1.call-start = ((), (), s32[]{:S(2)}) async-start(), calls=%async_computation.1 | async-start | bytes 5570560 | tf_op jit(solution)/shard_map/all_gather | solution.py:174
  8.2 7.8 %collective-permute-start = (bf16[1,2,8,4096]{3,2,1,0:T(8,128)(2,1)S(1)}, bf16[1,2,8,4096]{3,2,1,0:T(8,128)(2,1)S(1)}, u32[]{:S(2)}, u32[]{:S(2)}) collective-permute-start(bf16[1,2,8,4096]{3,2,1,0:T(8,128)(2,1)S(1)} %get-tuple-element.32), channel_id=1, source_target_pairs={{0,16},{16,32},{32,48},{48,64},{64,80},{80,96},{96,112},{1,17},{17... | collective-permute-start | bytes 393224 | tf_op jit(solution)/shard_map/ppermute | solution.py:28
  13.8 10.4 %copy-start = (s32[16,4]{0,1:T(4,128)S(1)}, s32[16,4]{0,1:T(4,128)}, u32[]{:S(2)}) copy-start(s32[16,4]{0,1:T(4,128)} %param.6) | copy-start | bytes 772
  13.8 11.2 %copy-start.1 = (s32[16,4]{0,1:T(4,128)S(1)}, s32[16,4]{0,1:T(4,128)}, u32[]{:S(2)}) copy-start(s32[16,4]{0,1:T(4,128)} %param.7) | copy-start | bytes 772
  13.9 7.2 %collective-permute-start.1 = (bf16[1,2,8,4096]{3,2,1,0:T(8,128)(2,1)S(1)}, bf16[1,2,8,4096]{3,2,1,0:T(8,128)(2,1)S(1)}, u32[]{:S(2)}, u32[]{:S(2)}) collective-permute-start(bf16[1,2,8,4096]{3,2,1,0:T(8,128)(2,1)S(1)} %get-tuple-element.33), channel_id=1, source_target_pairs={{16,0},{32,16},{48,32},{64,48},{80,64},{96,80},{112,96},{17,1},{33... | collective-permute-start | bytes 393224 | tf_op jit(solution)/shard_map/ppermute | solution.py:30
  23.5 84.6 %all-gather.5.cloned.1.call-start = ((), (), s32[]{:S(2)}) async-start(), calls=%async_computation | async-start | bytes 5570560 | tf_op jit(solution)/shard_map/all_gather | solution.py:174
  24.2 125.2 %all-gather.11.cloned.1.call-start = ((), (), s32[]{:S(2)}) async-start(), calls=%async_computation.3 | async-start | bytes 5570560 | tf_op jit(solution)/shard_map/all_gather | solution.py:182
  99.5 91.4 %all-gather.9.cloned.1.call-start = ((), (), s32[]{:S(2)}) async-start(), calls=%async_computation.2 | async-start | bytes 5570560 | tf_op jit(solution)/shard_map/all_gather | solution.py:182
Sparse Core Ops, SparseCore 0:
  23.6 43.0 all-gather.6
  68.4 39.6 all-gather.4
  109.8 39.6 all-gather.10
  151.0 39.7 all-gather.8

commit v3 on v2

--- a/solution.py
+++ b/solution.py
@@ -12,7 +12,8 @@
 LANES = 128
 BLOCK_COLS = 512
 CHUNK_ROWS = 32
-GATHER_COLS = 1024
+SPLIT_BASE = 16
+SPLIT = (10,)
 COST_SCALE = 1000
 LOOKAHEAD = 2
 
@@ -114,7 +115,7 @@
         copy.wait()
 
 
-def chunk_call(mid, left, rs, cs, psi_acc, phi_acc, *, index, count, rows_out):
+def chunk_call(mid, prev, rs, cs, psi_acc, phi_acc, *, index, count, start, rows_out):
     epochs, images, rows_in, chunk = mid.shape
     hyps = psi_acc.shape[0]
     cols = psi_acc.shape[2]
@@ -123,23 +124,24 @@
     last = index == count - 1
     out_lo = side if first else side - LANES
     out_hi = side + chunk if last else side + chunk - LANES
-    col_base = index * chunk - side
+    col_base = start - side
     kernel = functools.partial(
         chunk_kernel, first=first, last=last, epochs=epochs, hyps=hyps, rows_in=rows_in, rows_out=rows_out,
         chunk=chunk, out_lo=out_lo, out_hi=out_hi, col_base=col_base,
     )
     width = out_hi - out_lo
-    vmem = pltpu.MemorySpace.VMEM
+    prev_block = prev.shape[-1] // side - 1
     smem = pltpu.MemorySpace.SMEM
     flops = 2 * epochs * hyps * images * rows_out * width * COST_SCALE
     return pl.pallas_call(
         kernel,
+        grid=(1,),
         out_shape=[jax.ShapeDtypeStruct((hyps, rows_out, cols), jnp.float32)] * 2,
         in_specs=[
             pl.BlockSpec(memory_space=smem),
             pl.BlockSpec(memory_space=smem),
-            pl.BlockSpec(memory_space=vmem),
-            pl.BlockSpec(memory_space=vmem),
+            pl.BlockSpec((epochs, images, rows_in, chunk), lambda i: (0, 0, 0, 0)),
+            pl.BlockSpec((epochs, images, rows_in, side), lambda i: (0, 0, 0, prev_block)),
             pl.BlockSpec(memory_space=pl.ANY),
             pl.BlockSpec(memory_space=pl.ANY),
         ],
@@ -150,13 +152,13 @@
             pltpu.SemaphoreType.DMA((2,)),
         ],
         input_output_aliases={4: 0, 5: 1},
-        compiler_params=pltpu.CompilerParams(vmem_limit_bytes=60 * 1024 * 1024),
+        compiler_params=pltpu.CompilerParams(vmem_limit_bytes=63 * 1024 * 1024),
         cost_estimate=pl.CostEstimate(
             flops=flops, transcendentals=0,
-            bytes_accessed=(mid.size + left.size) * 2 + 2 * hyps * rows_out * width * 4,
+            bytes_accessed=mid.size * 2 + epochs * images * rows_in * side * 2 + 2 * hyps * rows_out * width * 4,
         ),
         name=f"shift_stack_{index}",
-    )(rs, cs, mid, left, psi_acc, phi_acc)
+    )(rs, cs, mid, prev, psi_acc, phi_acc)
 
 
 def body(psi, phi, row_shift, col_shift):
@@ -165,8 +167,9 @@
     hyp_count = row_shift.shape[1]
     images = jnp.stack([psi, phi], 1)
     extended = with_halo(images, (("sky", 2),), DEPTH)
-    count = col_count // GATHER_COLS
-    pieces = [extended[..., GATHER_COLS * i:GATHER_COLS * (i + 1)] for i in range(count)]
+    bounds = [0] + [b * col_count // SPLIT_BASE for b in SPLIT] + [col_count]
+    count = len(bounds) - 1
+    pieces = [extended[..., bounds[i]:bounds[i + 1]] for i in range(count)]
     rs = row_shift.reshape(-1)
     cs = col_shift.reshape(-1)
     psi_acc = jnp.zeros((hyp_count, row_count, col_count), jnp.float32)
@@ -174,8 +177,10 @@
     gathered = [lax.all_gather(pieces[i], "epoch", axis=0, tiled=True) for i in range(min(LOOKAHEAD, count))]
     for i in range(count):
         mid = gathered[i]
-        left = gathered[i - 1][..., GATHER_COLS - 2 * LANES:] if i > 0 else mid[..., :2 * LANES]
-        psi_acc, phi_acc = chunk_call(mid, left, rs, cs, psi_acc, phi_acc, index=i, count=count, rows_out=row_count)
+        prev = gathered[i - 1] if i > 0 else mid
+        psi_acc, phi_acc = chunk_call(
+            mid, prev, rs, cs, psi_acc, phi_acc, index=i, count=count, start=bounds[i], rows_out=row_count
+        )
         ahead = i + LOOKAHEAD
         if ahead < count:
             piece, psi_acc, phi_acc = lax.optimization_barrier((pieces[ahead], psi_acc, phi_acc))

time: 231 us -> 215 us (0.931)
  local copies, waits for them, and re-layouts: 16 us -> 6.49 us
  Pallas kernels: 106 us -> 101 us
  waiting for transfers between devices: 84.5 us -> 81.7 us
    all_gather x2 -> x0, waiting for transfers between devices: 28.5 us -> none  [body(): gathered.append(lax.all_gather(piece, 'epoch', axis=0, tiled=True))]
    all_gather x2, waiting for transfers between devices: 49.4 us -> 75.8 us  [body(): lax.all_gather(pieces[i], 'epoch', axis=0, tiled=True)]
    slice x4 -> x0, local copies, waits for them, and re-layouts: 9.58 us -> none  [the longest x2 4.99 us: body(): gathered[i - 1][..., GATHER_COLS - 2 * LANES:]]
    pallas_call x4 -> x2, Pallas kernels: 106 us -> 101 us  [chunk_call(): pl.pallas_call(kernel, grid=(1,), out_shape=[jax.ShapeDtypeStruct((hyps,...]
  transfers between devices with their start and end apart: 6 -> 4, of which waited for: 6 -> 3; matrix products, arithmetic and copies ran while one was open for 6% -> 3% of each run, Pallas kernels for 32% -> 27%
where the time goes in v3:
time: 215 us; the launch traced here: 214 us
  Pallas kernels  101 us (47%)
  waiting for transfers between devices  81.7 us (38%)
  between operations  14.1 us (7%)
  starting transfers between devices  7.03 us (3%)
  local copies, waits for them, and re-layouts  6.49 us (3%)
  other arithmetic  3.87 us (2%)
    pallas_call x2, Pallas kernels, chunk_call(): pl.pallas_call(kernel, grid=(1,), out_shape=[jax.ShapeDtypeStruct((hyps,...  101 us
    all_gather x2, waiting for transfers between devices, body(): lax.all_gather(pieces[i], 'epoch', axis=0, tiled=True)  75.8 us
    ppermute x1, starting transfers between devices, with_halo(): lax.ppermute(tail, axis, [(i, (i + 1) % count) for i in range(ends)])  5.66 us
    ppermute x1, waiting for transfers between devices, with_halo(): lax.ppermute(head, axis, [((i + 1) % count, i) for i in range(ends)])  5.08 us
    another operation x2, local copies, waits for them, and re-layouts  5 us
  transfers between devices with their start and end apart: 4, of which 3 were waited for; matrix products, arithmetic and copies ran while one was open for 3% of the time, Pallas kernels for 27%

profile of v3, /device:TPU:1, one launch (start us, length us, event | category | flops | bytes accessed | tf_op | source)
XLA Modules:
  0.0 214.4 jit_solution(13219094542498507116)
XLA Ops:
  7.2 0.0 copy-start
  7.2 0.0 copy-start.1
  7.2 0.0 copy-start.2
  7.2 0.0 copy-start.3
  7.2 0.0 all-gather.5.cloned.1.call-start
  7.3 1.0 pad_maximum_fusion.5
  8.3 5.7 %collective-permute-start = (bf16[1,2,8,4096]{3,2,1,0:T(8,128)(2,1)S(1)}, bf16[1,2,8,4096]{3,2,1,0:T(8,128)(2,1)S(1)}, u32[]{:S(2)}, u32[]{:S(2)}) collective-permute-start(bf16[1,2,8,4096]{3,2,1,0:T(8,128)(2,1)S(1)} %get-tuple-element.6), channel_id=1, source_target_pairs={{0,16},{16,32},{32,48},{48,64},{64,80},{80,96},{96,112},{1,17},{17... | collective-permute-start | bytes 393224 | tf_op jit(solution)/shard_map/ppermute | solution.py:29
  13.9 1.3 collective-permute-start.1
  15.2 0.8 collective-permute-done
  16.1 5.1 %collective-permute-done.1 = bf16[1,2,8,4096]{3,2,1,0:T(8,128)(2,1)S(1)} collective-permute-done((bf16[1,2,8,4096]{3,2,1,0:T(8,128)(2,1)S(1)}, bf16[1,2,8,4096]{3,2,1,0:T(8,128)(2,1)S(1)}, u32[]{:S(2)}, u32[]{:S(2)}) %collective-permute-start.1) | collective-permute-done | bytes 131104 | tf_op jit(solution)/shard_map/ppermute | solution.py:31
  21.2 2.0 pad_maximum_fusion
  23.2 0.0 all-gather.5.cloned.1.call-update
  23.2 0.0 all-gather.3.cloned.1.call-start
  23.3 0.0 copy-done
  23.3 0.0 copy-done.1
  23.3 0.8 pad_maximum_fusion.3
  24.1 0.0 all-gather.3.cloned.1.call-update
  24.1 0.0 copy-done.2
  24.1 0.1 copy.14
  24.2 0.7 reshape.10.rs_ref
  24.9 0.0 copy-done.3
  24.9 0.1 copy.15
  25.0 0.6 reshape.11.cs_ref
  25.6 75.8 %all-gather.5.cloned.1.call-done.mid_ref.left_ref = bf16[16,2,80,2560]{3,2,1,0:T(8,128)(2,1)} async-done(((bf16[1,2,80,2560]{3,2,1,0:T(8,128)(2,1)}), bf16[16,2,80,2560]{3,2,1,0:T(8,128)(2,1)}) %all-gather.5.cloned.1.call-update) | async-done | bytes 13107216 | tf_op jit(solution)/shard_map/all_gather | solution.py:177
  101.4 2.5 %broadcast_1_psi_in_phi_in.2.clone.phi_in = f32[4,64,4096]{2,1,0:T(8,128)} broadcast(f32[]{:T(128)} %constant.0.clone.1), dimensions={} | broadcast | bytes 4194308 | tf_op jit(solution)/shard_map/broadcast.1.psi_in.phi_in
  103.9 2.5 %broadcast_1_psi_in_phi_in.2.psi_in = f32[4,64,4096]{2,1,0:T(8,128)} broadcast(f32[]{:T(128)} %constant.0.clone.1), dimensions={} | broadcast | bytes 4194308 | tf_op jit(solution)/shard_map/broadcast.1.psi_in.phi_in
  106.4 57.3 %shift_stack_0.1 = (f32[4,64,4096]{2,1,0:T(8,128)}, f32[4,64,4096]{2,1,0:T(8,128)}) custom-call(s32[64]{0:T(128)} %reshape.10.rs_ref, s32[64]{0:T(128)} %reshape.11.cs_ref, bf16[16,2,80,2560]{3,2,1,0:T(8,128)(2,1)} %all-gather.5.cloned.1.call-done.mid_ref.left_ref, ...), custom_call_target="tpu_custom_call", output_to_operand_aliasing={{0}: (4, {}), {1}: (5, {})} | custom-call | flops 39845888000 | bytes 19398656 | tf_op jit(solution)/shard_map/shift_stack_0/pallas_call | solution.py:136
  163.7 0.0 all-gather.3.cloned.1.call-done.mid_ref
  163.7 43.8 %shift_stack_1.1 = (f32[4,64,4096]{2,1,0:T(8,128)}, f32[4,64,4096]{2,1,0:T(8,128)}) custom-call(s32[64]{0:T(128)} %reshape.10.rs_ref, s32[64]{0:T(128)} %reshape.11.cs_ref, bf16[16,2,80,1536]{3,2,1,0:T(8,128)(2,1)} %all-gather.3.cloned.1.call-done.mid_ref, ...), custom_call_target="tpu_custom_call", output_to_operand_aliasing={{0}: (4, {}), {1}: (5, {})} | custom-call | flops 27262976000 | bytes 12582912 | tf_op jit(solution)/shard_map/shift_stack_1/pallas_call | solution.py:136
Async XLA Ops:
  7.2 16.1 %copy-start = (bf16[1,64,4096]{2,1,0:T(8,128)(2,1)S(1)}, bf16[1,64,4096]{2,1,0:T(8,128)(2,1)}, u32[]{:S(2)}) copy-start(bf16[1,64,4096]{2,1,0:T(8,128)(2,1)} %param.5) | copy-start | bytes 1572868
  7.2 16.1 %copy-start.1 = (bf16[1,64,4096]{2,1,0:T(8,128)(2,1)S(1)}, bf16[1,64,4096]{2,1,0:T(8,128)(2,1)}, u32[]{:S(2)}) copy-start(bf16[1,64,4096]{2,1,0:T(8,128)(2,1)} %param.4) | copy-start | bytes 1572868
  7.2 16.9 %copy-start.2 = (s32[16,4]{0,1:T(4,128)S(1)}, s32[16,4]{0,1:T(4,128)}, u32[]{:S(2)}) copy-start(s32[16,4]{0,1:T(4,128)} %param.6) | copy-start | bytes 772
  7.2 17.7 %copy-start.3 = (s32[16,4]{0,1:T(4,128)S(1)}, s32[16,4]{0,1:T(4,128)}, u32[]{:S(2)}) copy-start(s32[16,4]{0,1:T(4,128)} %param.7) | copy-start | bytes 772
  7.2 94.2 %all-gather.5.cloned.1.call-start = ((), (), s32[]{:S(2)}) async-start(), calls=%async_computation.1 | async-start | bytes 13926400 | tf_op jit(solution)/shard_map/all_gather | solution.py:177
  8.3 7.8 %collective-permute-start = (bf16[1,2,8,4096]{3,2,1,0:T(8,128)(2,1)S(1)}, bf16[1,2,8,4096]{3,2,1,0:T(8,128)(2,1)S(1)}, u32[]{:S(2)}, u32[]{:S(2)}) collective-permute-start(bf16[1,2,8,4096]{3,2,1,0:T(8,128)(2,1)S(1)} %get-tuple-element.6), channel_id=1, source_target_pairs={{0,16},{16,32},{32,48},{48,64},{64,80},{80,96},{96,112},{1,17},{17... | collective-permute-start | bytes 393224 | tf_op jit(solution)/shard_map/ppermute | solution.py:29
  13.9 7.2 %collective-permute-start.1 = (bf16[1,2,8,4096]{3,2,1,0:T(8,128)(2,1)S(1)}, bf16[1,2,8,4096]{3,2,1,0:T(8,128)(2,1)S(1)}, u32[]{:S(2)}, u32[]{:S(2)}) collective-permute-start(bf16[1,2,8,4096]{3,2,1,0:T(8,128)(2,1)S(1)} %get-tuple-element.7), channel_id=1, source_target_pairs={{16,0},{32,16},{48,32},{64,48},{80,64},{96,80},{112,96},{17,1},{33... | collective-permute-start | bytes 393224 | tf_op jit(solution)/shard_map/ppermute | solution.py:31
  23.2 140.5 %all-gather.3.cloned.1.call-start = ((), (), s32[]{:S(2)}) async-start(), calls=%async_computation | async-start | bytes 8355840 | tf_op jit(solution)/shard_map/all_gather | solution.py:177
Sparse Core Ops, SparseCore 0:
  23.3 77.9 all-gather.4
  103.1 50.6 all-gather.2

commit v4 on v3

--- a/solution.py
+++ b/solution.py
@@ -13,7 +13,7 @@
 BLOCK_COLS = 512
 CHUNK_ROWS = 32
 SPLIT_BASE = 16
-SPLIT = (10,)
+SPLIT = (6, 12)
 COST_SCALE = 1000
 LOOKAHEAD = 2
 
@@ -37,7 +37,6 @@
 
 def chunk_kernel(rs_ref, cs_ref, mid_ref, left_ref, psi_in, phi_in, psi_hbm, phi_hbm, slab_ref, out_vmem, sems,
                  *, first, last, epochs, hyps, rows_in, rows_out, chunk, out_lo, out_hi, col_base):
-    del psi_in, phi_in
     side = left_ref.shape[-1]
     slab_rows = slab_ref.shape[1]
     slab_cols = slab_ref.shape[2]
@@ -115,10 +114,8 @@
         copy.wait()
 
 
-def chunk_call(mid, prev, rs, cs, psi_acc, phi_acc, *, index, count, start, rows_out):
+def chunk_call(mid, prev, rs, cs, psi_acc, phi_acc, *, index, count, start, rows_out, hyps, cols):
     epochs, images, rows_in, chunk = mid.shape
-    hyps = psi_acc.shape[0]
-    cols = psi_acc.shape[2]
     side = 2 * LANES
     first = index == 0
     last = index == count - 1
@@ -129,6 +126,12 @@
         chunk_kernel, first=first, last=last, epochs=epochs, hyps=hyps, rows_in=rows_in, rows_out=rows_out,
         chunk=chunk, out_lo=out_lo, out_hi=out_hi, col_base=col_base,
     )
+    if psi_acc is None:
+        body_kernel = kernel
+
+        def kernel(rs_ref, cs_ref, mid_ref, left_ref, psi_hbm, phi_hbm, *scratch):
+            body_kernel(rs_ref, cs_ref, mid_ref, left_ref, None, None, psi_hbm, phi_hbm, *scratch)
+
     width = out_hi - out_lo
     prev_block = prev.shape[-1] // side - 1
     smem = pltpu.MemorySpace.SMEM
@@ -142,23 +145,21 @@
             pl.BlockSpec(memory_space=smem),
             pl.BlockSpec((epochs, images, rows_in, chunk), lambda i: (0, 0, 0, 0)),
             pl.BlockSpec((epochs, images, rows_in, side), lambda i: (0, 0, 0, prev_block)),
-            pl.BlockSpec(memory_space=pl.ANY),
-            pl.BlockSpec(memory_space=pl.ANY),
-        ],
+        ] + ([] if psi_acc is None else [pl.BlockSpec(memory_space=pl.ANY)] * 2),
         out_specs=[pl.BlockSpec(memory_space=pl.ANY), pl.BlockSpec(memory_space=pl.ANY)],
         scratch_shapes=[
             pltpu.VMEM((epochs, rows_in + 8, side + chunk + LANES), jnp.float32),
             pltpu.VMEM((images, hyps, rows_out, chunk + LANES), jnp.float32),
             pltpu.SemaphoreType.DMA((2,)),
         ],
-        input_output_aliases={4: 0, 5: 1},
+        input_output_aliases={} if psi_acc is None else {4: 0, 5: 1},
         compiler_params=pltpu.CompilerParams(vmem_limit_bytes=63 * 1024 * 1024),
         cost_estimate=pl.CostEstimate(
             flops=flops, transcendentals=0,
             bytes_accessed=mid.size * 2 + epochs * images * rows_in * side * 2 + 2 * hyps * rows_out * width * 4,
         ),
         name=f"shift_stack_{index}",
-    )(rs, cs, mid, prev, psi_acc, phi_acc)
+    )(rs, cs, mid, prev, *([] if psi_acc is None else [psi_acc, phi_acc]))
 
 
 def body(psi, phi, row_shift, col_shift):
@@ -172,14 +173,14 @@
     pieces = [extended[..., bounds[i]:bounds[i + 1]] for i in range(count)]
     rs = row_shift.reshape(-1)
     cs = col_shift.reshape(-1)
-    psi_acc = jnp.zeros((hyp_count, row_count, col_count), jnp.float32)
-    phi_acc = jnp.zeros((hyp_count, row_count, col_count), jnp.float32)
+    psi_acc = phi_acc = None
     gathered = [lax.all_gather(pieces[i], "epoch", axis=0, tiled=True) for i in range(min(LOOKAHEAD, count))]
     for i in range(count):
         mid = gathered[i]
         prev = gathered[i - 1] if i > 0 else mid
         psi_acc, phi_acc = chunk_call(
-            mid, prev, rs, cs, psi_acc, phi_acc, index=i, count=count, start=bounds[i], rows_out=row_count
+            mid, prev, rs, cs, psi_acc, phi_acc, index=i, count=count, start=bounds[i], rows_out=row_count,
+            hyps=hyp_count, cols=col_count,
         )
         ahead = i + LOOKAHEAD
         if ahead < count:

time: 215 us -> 211 us (0.981)
  local copies, waits for them, and re-layouts: 6.49 us -> 1.46 us
  Pallas kernels: 101 us -> 104 us
    all_gather x2, waiting for transfers between devices: 75.8 us -> 67.8 us  [body(): lax.all_gather(pieces[i], 'epoch', axis=0, tiled=True)]
    all_gather x0 -> x1, waiting for transfers between devices: none -> 6.49 us  [body(): gathered.append(lax.all_gather(piece, 'epoch', axis=0, tiled=True))]
    another operation x2 -> x0, local copies, waits for them, and re-layouts: 5 us -> none
    pallas_call x2 -> x3, Pallas kernels: 101 us -> 104 us  [chunk_call(): pl.pallas_call(kernel, grid=(1,), out_shape=[jax.ShapeDtypeStruct((hyps,...]
  transfers between devices with their start and end apart: 4 -> 5, of which waited for: 3 -> 5; matrix products, arithmetic and copies ran while one was open for 3% -> 1% of each run, Pallas kernels for 27% -> 34%
where the time goes in v4:
time: 211 us
  Pallas kernels  104 us (49%)
  waiting for transfers between devices  80.9 us (38%)
  between operations  13.8 us (7%)
  starting transfers between devices  7.06 us (3%)
  other arithmetic  4.04 us (2%)
    pallas_call x3, Pallas kernels, chunk_call(): pl.pallas_call(kernel, grid=(1,), out_shape=[jax.ShapeDtypeStruct((hyps,...  104 us
    all_gather x2, waiting for transfers between devices, body(): lax.all_gather(pieces[i], 'epoch', axis=0, tiled=True)  67.8 us
    all_gather x1, waiting for transfers between devices, body(): gathered.append(lax.all_gather(piece, 'epoch', axis=0, tiled=True))  6.49 us
    ppermute x1, starting transfers between devices, with_halo(): lax.ppermute(tail, axis, [(i, (i + 1) % count) for i in range(ends)])  5.66 us
    ppermute x1, waiting for transfers between devices, with_halo(): lax.ppermute(head, axis, [((i + 1) % count, i) for i in range(ends)])  5.08 us
  transfers between devices with their start and end apart: 5, of which 5 were waited for; matrix products, arithmetic and copies ran while one was open for 1% of the time, Pallas kernels for 34%

profile of v4, /device:TPU:1, one launch (start us, length us, event | category | flops | bytes accessed | tf_op | source)
XLA Modules:
  0.0 210.8 jit_solution(15827256750449554851)
XLA Ops:
  7.2 0.0 copy-start.1
  7.2 0.0 copy-start
  7.2 0.0 copy-start.2
  7.2 0.0 copy-start.3
  7.2 0.0 all-gather.4.cloned.1.call-start
  7.3 1.0 pad_maximum_fusion.6
  8.3 5.7 %collective-permute-start = (bf16[1,2,8,4096]{3,2,1,0:T(8,128)(2,1)S(1)}, bf16[1,2,8,4096]{3,2,1,0:T(8,128)(2,1)S(1)}, u32[]{:S(2)}, u32[]{:S(2)}) collective-permute-start(bf16[1,2,8,4096]{3,2,1,0:T(8,128)(2,1)S(1)} %get-tuple-element.18), channel_id=1, source_target_pairs={{0,16},{16,32},{32,48},{48,64},{64,80},{80,96},{96,112},{1,17},{17... | collective-permute-start | bytes 393224 | tf_op jit(solution)/shard_map/ppermute | solution.py:29
  14.0 1.3 collective-permute-start.1
  15.3 0.8 collective-permute-done
  16.1 5.1 %collective-permute-done.1 = bf16[1,2,8,4096]{3,2,1,0:T(8,128)(2,1)S(1)} collective-permute-done((bf16[1,2,8,4096]{3,2,1,0:T(8,128)(2,1)S(1)}, bf16[1,2,8,4096]{3,2,1,0:T(8,128)(2,1)S(1)}, u32[]{:S(2)}, u32[]{:S(2)}) %collective-permute-start.1) | collective-permute-done | bytes 131104 | tf_op jit(solution)/shard_map/ppermute | solution.py:31
  21.2 2.2 %pad_maximum_fusion = (bf16[1,2,80,1536]{3,2,1,0:T(8,128)(2,1)}, bf16[1,2,80,1536]{3,2,1,0:T(8,128)(2,1)}) fusion(bf16[1,2,8,4096]{3,2,1,0:T(8,128)(2,1)S(1)} %collective-permute-done.1, bf16[1,2,8,4096]{3,2,1,0:T(8,128)(2,1)S(1)} %collective-permute-done, bf16[1,1,64,4096]{3,2,1,0:T(8,128)(2,1)} %bitcast.3, bf16[1,1,64,4096]{3,2,1,0:T(8,128)(2,1)} %bitcast.6), kind=kLoop, calls=%fused_computation | loop fusion | flops 3932160 | bytes 2293760 | tf_op jit(solution)/shard_map/concatenate | solution.py:27
  23.4 0.0 all-gather.4.cloned.1.call-update
  23.4 0.0 all-gather.8.cloned.1.call-start
  23.5 0.7 all-gather.8.cloned.1.call-update
  24.2 0.0 all-gather.6.cloned.1.call-start
  24.2 0.0 copy-done.2
  24.2 0.1 copy.14
  24.3 0.6 reshape.10.rs_ref
  25.0 0.0 copy-done.3
  25.0 0.1 copy.15
  25.0 0.6 reshape.11.cs_ref
  25.7 0.0 copy-done.1
  25.7 0.0 copy-done
  25.7 0.8 pad_maximum_fusion.4
  26.5 50.4 %all-gather.4.cloned.1.call-done.mid_ref.left_ref = bf16[16,2,80,1536]{3,2,1,0:T(8,128)(2,1)} async-done(((bf16[1,2,80,1536]{3,2,1,0:T(8,128)(2,1)}), bf16[16,2,80,1536]{3,2,1,0:T(8,128)(2,1)}) %all-gather.4.cloned.1.call-update) | async-done | bytes 7864336 | tf_op jit(solution)/shard_map/all_gather | solution.py:177
  76.9 35.1 %shift_stack_0.1 = (f32[4,64,4096]{2,1,0:T(8,128)}, f32[4,64,4096]{2,1,0:T(8,128)}) custom-call(s32[64]{0:T(128)} %reshape.10.rs_ref, s32[64]{0:T(128)} %reshape.11.cs_ref, bf16[16,2,80,1536]{3,2,1,0:T(8,128)(2,1)} %all-gather.4.cloned.1.call-done.mid_ref.left_ref, bf16[16,2,80,1536]{3,2,1,0:T(8,128)(2,1)} %all-gather.4.cloned.1.call-done.mid_ref.left_ref), custom_call_target="tpu_custom_call" | custom-call | flops 23068672000 | bytes 12058624 | tf_op jit(solution)/shard_map/shift_stack_0/pallas_call | solution.py:139
  112.0 0.0 all-gather.6.cloned.1.call-update
  112.0 17.3 %all-gather.8.cloned.1.call-done.mid_ref.left_ref = bf16[16,2,80,1536]{3,2,1,0:T(8,128)(2,1)} async-done(((bf16[1,2,80,1536]{3,2,1,0:T(8,128)(2,1)}), bf16[16,2,80,1536]{3,2,1,0:T(8,128)(2,1)}) %all-gather.8.cloned.1.call-update) | async-done | bytes 7864336 | tf_op jit(solution)/shard_map/all_gather | solution.py:177
  129.3 35.9 %shift_stack_1.1 = (f32[4,64,4096]{2,1,0:T(8,128)}, f32[4,64,4096]{2,1,0:T(8,128)}) custom-call(s32[64]{0:T(128)} %reshape.10.rs_ref, s32[64]{0:T(128)} %reshape.11.cs_ref, bf16[16,2,80,1536]{3,2,1,0:T(8,128)(2,1)} %all-gather.8.cloned.1.call-done.mid_ref.left_ref, ...), custom_call_target="tpu_custom_call", output_to_operand_aliasing={{0}: (4, {}), {1}: (5, {})} | custom-call | flops 25165824000 | bytes 12320768 | tf_op jit(solution)/shard_map/shift_stack_1/pallas_call | solution.py:139
  165.2 6.5 %all-gather.6.cloned.1.call-done.mid_ref = bf16[16,2,80,1024]{3,2,1,0:T(8,128)(2,1)} async-done(((bf16[1,2,80,1024]{3,2,1,0:T(8,128)(2,1)}), bf16[16,2,80,1024]{3,2,1,0:T(8,128)(2,1)}) %all-gather.6.cloned.1.call-update) | async-done | bytes 5242896 | tf_op jit(solution)/shard_map/all_gather | solution.py:188
  171.7 32.6 %shift_stack_2.1 = (f32[4,64,4096]{2,1,0:T(8,128)}, f32[4,64,4096]{2,1,0:T(8,128)}) custom-call(s32[64]{0:T(128)} %reshape.10.rs_ref, s32[64]{0:T(128)} %reshape.11.cs_ref, bf16[16,2,80,1024]{3,2,1,0:T(8,128)(2,1)} %all-gather.6.cloned.1.call-done.mid_ref, ...), custom_call_target="tpu_custom_call", output_to_operand_aliasing={{0}: (4, {}), {1}: (5, {})} | custom-call | flops 18874368000 | bytes 8912896 | tf_op jit(solution)/shard_map/shift_stack_2/pallas_call | solution.py:139
Async XLA Ops:
  7.2 18.5 %copy-start.1 = (bf16[1,64,4096]{2,1,0:T(8,128)(2,1)S(1)}, bf16[1,64,4096]{2,1,0:T(8,128)(2,1)}, u32[]{:S(2)}) copy-start(bf16[1,64,4096]{2,1,0:T(8,128)(2,1)} %param.4) | copy-start | bytes 1572868
  7.2 18.5 %copy-start = (bf16[1,64,4096]{2,1,0:T(8,128)(2,1)S(1)}, bf16[1,64,4096]{2,1,0:T(8,128)(2,1)}, u32[]{:S(2)}) copy-start(bf16[1,64,4096]{2,1,0:T(8,128)(2,1)} %param.5) | copy-start | bytes 1572868
  7.2 17.1 %copy-start.2 = (s32[16,4]{0,1:T(4,128)S(1)}, s32[16,4]{0,1:T(4,128)}, u32[]{:S(2)}) copy-start(s32[16,4]{0,1:T(4,128)} %param.6) | copy-start | bytes 772
  7.2 17.8 %copy-start.3 = (s32[16,4]{0,1:T(4,128)S(1)}, s32[16,4]{0,1:T(4,128)}, u32[]{:S(2)}) copy-start(s32[16,4]{0,1:T(4,128)} %param.7) | copy-start | bytes 772
  7.2 69.7 %all-gather.4.cloned.1.call-start = ((), (), s32[]{:S(2)}) async-start(), calls=%async_computation | async-start | bytes 8355840 | tf_op jit(solution)/shard_map/all_gather | solution.py:177
  8.3 7.8 %collective-permute-start = (bf16[1,2,8,4096]{3,2,1,0:T(8,128)(2,1)S(1)}, bf16[1,2,8,4096]{3,2,1,0:T(8,128)(2,1)S(1)}, u32[]{:S(2)}, u32[]{:S(2)}) collective-permute-start(bf16[1,2,8,4096]{3,2,1,0:T(8,128)(2,1)S(1)} %get-tuple-element.18), channel_id=1, source_target_pairs={{0,16},{16,32},{32,48},{48,64},{64,80},{80,96},{96,112},{1,17},{17... | collective-permute-start | bytes 393224 | tf_op jit(solution)/shard_map/ppermute | solution.py:29
  14.0 7.2 %collective-permute-start.1 = (bf16[1,2,8,4096]{3,2,1,0:T(8,128)(2,1)S(1)}, bf16[1,2,8,4096]{3,2,1,0:T(8,128)(2,1)S(1)}, u32[]{:S(2)}, u32[]{:S(2)}) collective-permute-start(bf16[1,2,8,4096]{3,2,1,0:T(8,128)(2,1)S(1)} %get-tuple-element.19), channel_id=1, source_target_pairs={{16,0},{32,16},{48,32},{64,48},{80,64},{96,80},{112,96},{17,1},{33... | collective-permute-start | bytes 393224 | tf_op jit(solution)/shard_map/ppermute | solution.py:31
  23.4 105.9 %all-gather.8.cloned.1.call-start = ((), (), s32[]{:S(2)}) async-start(), calls=%async_computation.2 | async-start | bytes 8355840 | tf_op jit(solution)/shard_map/all_gather | solution.py:177
  24.2 147.5 %all-gather.6.cloned.1.call-start = ((), (), s32[]{:S(2)}) async-start(), calls=%async_computation.1 | async-start | bytes 5570560 | tf_op jit(solution)/shard_map/all_gather | solution.py:188
Sparse Core Ops, SparseCore 0:
  23.6 53.2 all-gather.3
  78.6 50.7 all-gather.7
  131.1 40.6 all-gather.5

commit v5 on v4

--- a/solution.py
+++ b/solution.py
@@ -13,7 +13,7 @@
 BLOCK_COLS = 512
 CHUNK_ROWS = 32
 SPLIT_BASE = 16
-SPLIT = (6, 12)
+SPLIT = (8, 13)
 COST_SCALE = 1000
 LOOKAHEAD = 2
 

time: 211 us -> 206 us (0.976)
  waiting for transfers between devices: 80.9 us -> 74.7 us
    all_gather x2, waiting for transfers between devices: 67.8 us -> 62.7 us  [body(): lax.all_gather(pieces[i], 'epoch', axis=0, tiled=True)]
  transfers between devices with their start and end apart: 5 -> 5, of which waited for: 5 -> 4; matrix products, arithmetic and copies ran while one was open for 1% -> 1% of each run, Pallas kernels for 34% -> 39%
where the time goes in v5:
time: 206 us
  Pallas kernels  104 us (50%)
  waiting for transfers between devices  74.7 us (36%)
  between operations  13.9 us (7%)
  starting transfers between devices  7.2 us (3%)
  other arithmetic  3.77 us (2%)
  local copies, waits for them, and re-layouts  2.37 us (1%)
    pallas_call x3, Pallas kernels, chunk_call(): pl.pallas_call(kernel, grid=(1,), out_shape=[jax.ShapeDtypeStruct((hyps,...  104 us
    all_gather x2, waiting for transfers between devices, body(): lax.all_gather(pieces[i], 'epoch', axis=0, tiled=True)  62.7 us
    all_gather x1, waiting for transfers between devices, body(): gathered.append(lax.all_gather(piece, 'epoch', axis=0, tiled=True))  6.06 us
    ppermute x1, starting transfers between devices, with_halo(): lax.ppermute(tail, axis, [(i, (i + 1) % count) for i in range(ends)])  5.79 us
    ppermute x1, waiting for transfers between devices, with_halo(): lax.ppermute(head, axis, [((i + 1) % count, i) for i in range(ends)])  5.08 us
  transfers between devices with their start and end apart: 5, of which 4 were waited for; matrix products, arithmetic and copies ran while one was open for 1% of the time, Pallas kernels for 39%

profile of v5, /device:TPU:1, one launch (start us, length us, event | category | flops | bytes accessed | tf_op | source)
XLA Modules:
  0.0 205.5 jit_solution(6067080065087975044)
XLA Ops:
  7.2 0.0 all-gather.4.cloned.1.call-start
  7.2 1.0 pad_maximum_fusion.4
  8.2 0.0 copy-start
  8.2 0.0 copy-start.1
  8.2 5.8 %collective-permute-start = (bf16[1,2,8,4096]{3,2,1,0:T(8,128)(2,1)S(1)}, bf16[1,2,8,4096]{3,2,1,0:T(8,128)(2,1)S(1)}, u32[]{:S(2)}, u32[]{:S(2)}) collective-permute-start(bf16[1,2,8,4096]{3,2,1,0:T(8,128)(2,1)S(1)} %get-tuple-element.16), channel_id=1, source_target_pairs={{0,16},{16,32},{32,48},{48,64},{64,80},{80,96},{96,112},{1,17},{17... | collective-permute-start | bytes 393224 | tf_op jit(solution)/shard_map/ppermute | solution.py:29
  14.0 1.3 collective-permute-start.1
  15.3 0.8 collective-permute-done
  16.1 5.1 %collective-permute-done.1 = bf16[1,2,8,4096]{3,2,1,0:T(8,128)(2,1)S(1)} collective-permute-done((bf16[1,2,8,4096]{3,2,1,0:T(8,128)(2,1)S(1)}, bf16[1,2,8,4096]{3,2,1,0:T(8,128)(2,1)S(1)}, u32[]{:S(2)}, u32[]{:S(2)}) %collective-permute-start.1) | collective-permute-done | bytes 131104 | tf_op jit(solution)/shard_map/ppermute | solution.py:31
  21.2 1.3 pad_maximum_fusion
  22.5 0.0 copy-start.2
  22.5 0.0 copy-start.3
  22.5 0.9 slice.20
  23.4 0.0 all-gather.4.cloned.1.call-update
  23.4 0.0 all-gather.8.cloned.1.call-start
  23.5 0.0 copy-done
  23.5 0.0 copy-done.1
  23.5 0.8 pad_maximum_fusion.1
  24.3 0.0 all-gather.8.cloned.1.call-update
  24.3 0.0 all-gather.6.cloned.1.call-start
  24.4 0.0 copy-done.2
  24.4 0.1 copy.14
  24.5 0.6 reshape.10.rs_ref
  25.1 0.0 copy-done.3
  25.1 0.1 copy.15
  25.2 0.7 reshape.11.cs_ref
  25.8 0.7 pad_maximum_fusion.2
  26.6 62.7 %all-gather.4.cloned.1.call-done.mid_ref.left_ref = bf16[16,2,80,2048]{3,2,1,0:T(8,128)(2,1)} async-done(((bf16[1,2,80,2048]{3,2,1,0:T(8,128)(2,1)}), bf16[16,2,80,2048]{3,2,1,0:T(8,128)(2,1)}) %all-gather.4.cloned.1.call-update) | async-done | bytes 10485776 | tf_op jit(solution)/shard_map/all_gather | solution.py:177
  89.2 46.2 %shift_stack_0.1 = (f32[4,64,4096]{2,1,0:T(8,128)}, f32[4,64,4096]{2,1,0:T(8,128)}) custom-call(s32[64]{0:T(128)} %reshape.10.rs_ref, s32[64]{0:T(128)} %reshape.11.cs_ref, bf16[16,2,80,2048]{3,2,1,0:T(8,128)(2,1)} %all-gather.4.cloned.1.call-done.mid_ref.left_ref, bf16[16,2,80,2048]{3,2,1,0:T(8,128)(2,1)} %all-gather.4.cloned.1.call-done.mid_ref.left_ref), custom_call_target="tpu_custom_call" | custom-call | flops 31457280000 | bytes 15728640 | tf_op jit(solution)/shard_map/shift_stack_0/pallas_call | solution.py:139
  135.4 0.0 all-gather.6.cloned.1.call-update
  135.5 0.0 all-gather.8.cloned.1.call-done.mid_ref.left_ref
  135.5 34.0 %shift_stack_1.1 = (f32[4,64,4096]{2,1,0:T(8,128)}, f32[4,64,4096]{2,1,0:T(8,128)}) custom-call(s32[64]{0:T(128)} %reshape.10.rs_ref, s32[64]{0:T(128)} %reshape.11.cs_ref, bf16[16,2,80,1280]{3,2,1,0:T(8,128)(2,1)} %all-gather.8.cloned.1.call-done.mid_ref.left_ref, ...), custom_call_target="tpu_custom_call", output_to_operand_aliasing={{0}: (4, {}), {1}: (5, {})} | custom-call | flops 20971520000 | bytes 10485760 | tf_op jit(solution)/shard_map/shift_stack_1/pallas_call | solution.py:139
  169.5 6.1 %all-gather.6.cloned.1.call-done.mid_ref = bf16[16,2,80,768]{3,2,1,0:T(8,128)(2,1)} async-done(((bf16[1,2,80,768]{3,2,1,0:T(8,128)(2,1)}), bf16[16,2,80,768]{3,2,1,0:T(8,128)(2,1)}) %all-gather.6.cloned.1.call-update) | async-done | bytes 3932176 | tf_op jit(solution)/shard_map/all_gather | solution.py:188
  175.5 23.5 %shift_stack_2.1 = (f32[4,64,4096]{2,1,0:T(8,128)}, f32[4,64,4096]{2,1,0:T(8,128)}) custom-call(s32[64]{0:T(128)} %reshape.10.rs_ref, s32[64]{0:T(128)} %reshape.11.cs_ref, bf16[16,2,80,768]{3,2,1,0:T(8,128)(2,1)} %all-gather.6.cloned.1.call-done.mid_ref, ...), custom_call_target="tpu_custom_call", output_to_operand_aliasing={{0}: (4, {}), {1}: (5, {})} | custom-call | flops 14680064000 | bytes 7077888 | tf_op jit(solution)/shard_map/shift_stack_2/pallas_call | solution.py:139
Async XLA Ops:
  7.2 82.1 %all-gather.4.cloned.1.call-start = ((), (), s32[]{:S(2)}) async-start(), calls=%async_computation | async-start | bytes 11141120 | tf_op jit(solution)/shard_map/all_gather | solution.py:177
  8.2 15.3 %copy-start = (bf16[1,64,4096]{2,1,0:T(8,128)(2,1)S(1)}, bf16[1,64,4096]{2,1,0:T(8,128)(2,1)}, u32[]{:S(2)}) copy-start(bf16[1,64,4096]{2,1,0:T(8,128)(2,1)} %param.5) | copy-start | bytes 1572868
  8.2 15.3 %copy-start.1 = (bf16[1,64,4096]{2,1,0:T(8,128)(2,1)S(1)}, bf16[1,64,4096]{2,1,0:T(8,128)(2,1)}, u32[]{:S(2)}) copy-start(bf16[1,64,4096]{2,1,0:T(8,128)(2,1)} %param.4) | copy-start | bytes 1572868
  8.2 7.9 %collective-permute-start = (bf16[1,2,8,4096]{3,2,1,0:T(8,128)(2,1)S(1)}, bf16[1,2,8,4096]{3,2,1,0:T(8,128)(2,1)S(1)}, u32[]{:S(2)}, u32[]{:S(2)}) collective-permute-start(bf16[1,2,8,4096]{3,2,1,0:T(8,128)(2,1)S(1)} %get-tuple-element.16), channel_id=1, source_target_pairs={{0,16},{16,32},{32,48},{48,64},{64,80},{80,96},{96,112},{1,17},{17... | collective-permute-start | bytes 393224 | tf_op jit(solution)/shard_map/ppermute | solution.py:29
  14.0 7.2 %collective-permute-start.1 = (bf16[1,2,8,4096]{3,2,1,0:T(8,128)(2,1)S(1)}, bf16[1,2,8,4096]{3,2,1,0:T(8,128)(2,1)S(1)}, u32[]{:S(2)}, u32[]{:S(2)}) collective-permute-start(bf16[1,2,8,4096]{3,2,1,0:T(8,128)(2,1)S(1)} %get-tuple-element.17), channel_id=1, source_target_pairs={{16,0},{32,16},{48,32},{64,48},{80,64},{96,80},{112,96},{17,1},{33... | collective-permute-start | bytes 393224 | tf_op jit(solution)/shard_map/ppermute | solution.py:31
  22.5 1.9 copy-start.2
  22.5 2.6 %copy-start.3 = (s32[16,4]{0,1:T(4,128)S(1)}, s32[16,4]{0,1:T(4,128)}, u32[]{:S(2)}) copy-start(s32[16,4]{0,1:T(4,128)} %param.7) | copy-start | bytes 772
  23.4 112.1 %all-gather.8.cloned.1.call-start = ((), (), s32[]{:S(2)}) async-start(), calls=%async_computation.2 | async-start | bytes 6963200 | tf_op jit(solution)/shard_map/all_gather | solution.py:177
  24.3 151.2 %all-gather.6.cloned.1.call-start = ((), (), s32[]{:S(2)}) async-start(), calls=%async_computation.1 | async-start | bytes 4177920 | tf_op jit(solution)/shard_map/all_gather | solution.py:188
Sparse Core Ops, SparseCore 0:
  23.5 65.6 all-gather.3
  90.9 44.5 all-gather.7
  137.2 38.2 all-gather.5

commit v6 on v5

--- a/solution.py
+++ b/solution.py
@@ -16,6 +16,7 @@
 SPLIT = (8, 13)
 COST_SCALE = 1000
 LOOKAHEAD = 2
+UNROLL = 8
 
 
 def with_halo(cells, sides, width):
@@ -62,7 +63,7 @@
 
         lax.fori_loop(0, epochs, convert, 0)
 
-        for h in range(hyps):
+        def one_hyp(h, carry):
             for rchunk in range(rows_out // CHUNK_ROWS):
                 y0 = rchunk * CHUNK_ROWS
                 for base_o, pieces in subs:
@@ -98,11 +99,14 @@
                         return out
 
                     zero = [[jnp.zeros((8, LANES), jnp.float32) for _ in range(pieces)] for _ in range(row_vregs)]
-                    acc = lax.fori_loop(0, epochs, add_epoch, zero, unroll=4)
+                    acc = lax.fori_loop(0, epochs, add_epoch, zero, unroll=UNROLL)
                     for k in range(row_vregs):
                         for p in range(pieces):
                             lo = base_o - out_lo + LANES * p
                             out_vmem[img, h, pl.ds(y0 + 8 * k, 8), pl.ds(lo, LANES)] = acc[k][p]
+            return carry
+
+        lax.fori_loop(0, hyps, one_hyp, 0)
         copy = pltpu.make_async_copy(
             out_vmem.at[img, :, :, pl.ds(0, width)],
             out_hbm.at[:, :, pl.ds(col_base + out_lo, width)],

time: 206 us -> 201 us (0.976)
  Pallas kernels: 104 us -> 84.2 us
  waiting for transfers between devices: 74.7 us -> 89.9 us
    pallas_call x3, Pallas kernels: 104 us -> 84.2 us  [chunk_call(): pl.pallas_call(kernel, grid=(1,), out_shape=[jax.ShapeDtypeStruct((hyps,...]
    all_gather x2, waiting for transfers between devices: 62.7 us -> 71.4 us  [body(): lax.all_gather(pieces[i], 'epoch', axis=0, tiled=True)]
    all_gather x1, waiting for transfers between devices: 6.06 us -> 12.5 us  [body(): gathered.append(lax.all_gather(piece, 'epoch', axis=0, tiled=True))]
  transfers between devices with their start and end apart: 5 -> 5, of which waited for: 4 -> 5; matrix products, arithmetic and copies ran while one was open for 1% -> 1% of each run, Pallas kernels for 39% -> 32%
where the time goes in v6:
time: 201 us
  waiting for transfers between devices  89.9 us (45%)
  Pallas kernels  84.2 us (42%)
  between operations  13.9 us (7%)
  starting transfers between devices  7.2 us (4%)
  other arithmetic  3.77 us (2%)
  local copies, waits for them, and re-layouts  2.37 us (1%)
    pallas_call x3, Pallas kernels, chunk_call(): pl.pallas_call(kernel, grid=(1,), out_shape=[jax.ShapeDtypeStruct((hyps,...  84.2 us
    all_gather x2, waiting for transfers between devices, body(): lax.all_gather(pieces[i], 'epoch', axis=0, tiled=True)  71.4 us
    all_gather x1, waiting for transfers between devices, body(): gathered.append(lax.all_gather(piece, 'epoch', axis=0, tiled=True))  12.5 us
    ppermute x1, starting transfers between devices, with_halo(): lax.ppermute(tail, axis, [(i, (i + 1) % count) for i in range(ends)])  5.79 us
    ppermute x1, waiting for transfers between devices, with_halo(): lax.ppermute(head, axis, [((i + 1) % count, i) for i in range(ends)])  5.08 us
  transfers between devices with their start and end apart: 5, of which 5 were waited for; matrix products, arithmetic and copies ran while one was open for 1% of the time, Pallas kernels for 32%

profile of v6, /device:TPU:1, one launch (start us, length us, event | category | flops | bytes accessed | tf_op | source)
XLA Modules:
  0.0 201.2 jit_solution(5805457004510759971)
XLA Ops:
  7.2 0.0 all-gather.4.cloned.1.call-start
  7.2 1.0 pad_maximum_fusion.4
  8.2 0.0 copy-start
  8.2 0.0 copy-start.1
  8.2 5.8 %collective-permute-start = (bf16[1,2,8,4096]{3,2,1,0:T(8,128)(2,1)S(1)}, bf16[1,2,8,4096]{3,2,1,0:T(8,128)(2,1)S(1)}, u32[]{:S(2)}, u32[]{:S(2)}) collective-permute-start(bf16[1,2,8,4096]{3,2,1,0:T(8,128)(2,1)S(1)} %get-tuple-element.16), channel_id=1, source_target_pairs={{0,16},{16,32},{32,48},{48,64},{64,80},{80,96},{96,112},{1,17},{17... | collective-permute-start | bytes 393224 | tf_op jit(solution)/shard_map/ppermute | solution.py:30
  14.0 1.3 collective-permute-start.1
  15.3 0.8 collective-permute-done
  16.1 5.1 %collective-permute-done.1 = bf16[1,2,8,4096]{3,2,1,0:T(8,128)(2,1)S(1)} collective-permute-done((bf16[1,2,8,4096]{3,2,1,0:T(8,128)(2,1)S(1)}, bf16[1,2,8,4096]{3,2,1,0:T(8,128)(2,1)S(1)}, u32[]{:S(2)}, u32[]{:S(2)}) %collective-permute-start.1) | collective-permute-done | bytes 131104 | tf_op jit(solution)/shard_map/ppermute | solution.py:32
  21.2 1.3 pad_maximum_fusion
  22.5 0.0 copy-start.2
  22.5 0.0 copy-start.3
  22.5 0.9 slice.20
  23.4 0.0 all-gather.4.cloned.1.call-update
  23.4 0.0 all-gather.8.cloned.1.call-start
  23.5 0.0 copy-done
  23.5 0.0 copy-done.1
  23.5 0.8 pad_maximum_fusion.1
  24.3 0.0 all-gather.8.cloned.1.call-update
  24.3 0.0 all-gather.6.cloned.1.call-start
  24.4 0.0 copy-done.2
  24.4 0.1 copy.14
  24.5 0.6 reshape.10.rs_ref
  25.1 0.0 copy-done.3
  25.1 0.1 copy.15
  25.2 0.7 reshape.11.cs_ref
  25.8 0.7 pad_maximum_fusion.2
  26.6 62.7 %all-gather.4.cloned.1.call-done.mid_ref.left_ref = bf16[16,2,80,2048]{3,2,1,0:T(8,128)(2,1)} async-done(((bf16[1,2,80,2048]{3,2,1,0:T(8,128)(2,1)}), bf16[16,2,80,2048]{3,2,1,0:T(8,128)(2,1)}) %all-gather.4.cloned.1.call-update) | async-done | bytes 10485776 | tf_op jit(solution)/shard_map/all_gather | solution.py:181
  89.2 37.4 %shift_stack_0.1 = (f32[4,64,4096]{2,1,0:T(8,128)}, f32[4,64,4096]{2,1,0:T(8,128)}) custom-call(s32[64]{0:T(128)} %reshape.10.rs_ref, s32[64]{0:T(128)} %reshape.11.cs_ref, bf16[16,2,80,2048]{3,2,1,0:T(8,128)(2,1)} %all-gather.4.cloned.1.call-done.mid_ref.left_ref, bf16[16,2,80,2048]{3,2,1,0:T(8,128)(2,1)} %all-gather.4.cloned.1.call-done.mid_ref.left_ref), custom_call_target="tpu_custom_call" | custom-call | flops 31457280000 | bytes 15728640 | tf_op jit(solution)/shard_map/shift_stack_0/pallas_call | solution.py:143
  126.7 0.0 all-gather.6.cloned.1.call-update
  126.7 8.8 %all-gather.8.cloned.1.call-done.mid_ref.left_ref = bf16[16,2,80,1280]{3,2,1,0:T(8,128)(2,1)} async-done(((bf16[1,2,80,1280]{3,2,1,0:T(8,128)(2,1)}), bf16[16,2,80,1280]{3,2,1,0:T(8,128)(2,1)}) %all-gather.8.cloned.1.call-update) | async-done | bytes 6553616 | tf_op jit(solution)/shard_map/all_gather | solution.py:181
  135.5 27.5 %shift_stack_1.1 = (f32[4,64,4096]{2,1,0:T(8,128)}, f32[4,64,4096]{2,1,0:T(8,128)}) custom-call(s32[64]{0:T(128)} %reshape.10.rs_ref, s32[64]{0:T(128)} %reshape.11.cs_ref, bf16[16,2,80,1280]{3,2,1,0:T(8,128)(2,1)} %all-gather.8.cloned.1.call-done.mid_ref.left_ref, ...), custom_call_target="tpu_custom_call", output_to_operand_aliasing={{0}: (4, {}), {1}: (5, {})} | custom-call | flops 20971520000 | bytes 10485760 | tf_op jit(solution)/shard_map/shift_stack_1/pallas_call | solution.py:143
  163.0 12.5 %all-gather.6.cloned.1.call-done.mid_ref = bf16[16,2,80,768]{3,2,1,0:T(8,128)(2,1)} async-done(((bf16[1,2,80,768]{3,2,1,0:T(8,128)(2,1)}), bf16[16,2,80,768]{3,2,1,0:T(8,128)(2,1)}) %all-gather.6.cloned.1.call-update) | async-done | bytes 3932176 | tf_op jit(solution)/shard_map/all_gather | solution.py:192
  175.5 19.3 %shift_stack_2.1 = (f32[4,64,4096]{2,1,0:T(8,128)}, f32[4,64,4096]{2,1,0:T(8,128)}) custom-call(s32[64]{0:T(128)} %reshape.10.rs_ref, s32[64]{0:T(128)} %reshape.11.cs_ref, bf16[16,2,80,768]{3,2,1,0:T(8,128)(2,1)} %all-gather.6.cloned.1.call-done.mid_ref, ...), custom_call_target="tpu_custom_call", output_to_operand_aliasing={{0}: (4, {}), {1}: (5, {})} | custom-call | flops 14680064000 | bytes 7077888 | tf_op jit(solution)/shard_map/shift_stack_2/pallas_call | solution.py:143
Async XLA Ops:
  7.2 82.1 %all-gather.4.cloned.1.call-start = ((), (), s32[]{:S(2)}) async-start(), calls=%async_computation | async-start | bytes 11141120 | tf_op jit(solution)/shard_map/all_gather | solution.py:181
  8.2 15.3 %copy-start = (bf16[1,64,4096]{2,1,0:T(8,128)(2,1)S(1)}, bf16[1,64,4096]{2,1,0:T(8,128)(2,1)}, u32[]{:S(2)}) copy-start(bf16[1,64,4096]{2,1,0:T(8,128)(2,1)} %param.5) | copy-start | bytes 1572868
  8.2 15.3 %copy-start.1 = (bf16[1,64,4096]{2,1,0:T(8,128)(2,1)S(1)}, bf16[1,64,4096]{2,1,0:T(8,128)(2,1)}, u32[]{:S(2)}) copy-start(bf16[1,64,4096]{2,1,0:T(8,128)(2,1)} %param.4) | copy-start | bytes 1572868
  8.2 7.9 %collective-permute-start = (bf16[1,2,8,4096]{3,2,1,0:T(8,128)(2,1)S(1)}, bf16[1,2,8,4096]{3,2,1,0:T(8,128)(2,1)S(1)}, u32[]{:S(2)}, u32[]{:S(2)}) collective-permute-start(bf16[1,2,8,4096]{3,2,1,0:T(8,128)(2,1)S(1)} %get-tuple-element.16), channel_id=1, source_target_pairs={{0,16},{16,32},{32,48},{48,64},{64,80},{80,96},{96,112},{1,17},{17... | collective-permute-start | bytes 393224 | tf_op jit(solution)/shard_map/ppermute | solution.py:30
  14.0 7.2 %collective-permute-start.1 = (bf16[1,2,8,4096]{3,2,1,0:T(8,128)(2,1)S(1)}, bf16[1,2,8,4096]{3,2,1,0:T(8,128)(2,1)S(1)}, u32[]{:S(2)}, u32[]{:S(2)}) collective-permute-start(bf16[1,2,8,4096]{3,2,1,0:T(8,128)(2,1)S(1)} %get-tuple-element.17), channel_id=1, source_target_pairs={{16,0},{32,16},{48,32},{64,48},{80,64},{96,80},{112,96},{17,1},{33... | collective-permute-start | bytes 393224 | tf_op jit(solution)/shard_map/ppermute | solution.py:32
  22.5 1.9 copy-start.2
  22.5 2.6 %copy-start.3 = (s32[16,4]{0,1:T(4,128)S(1)}, s32[16,4]{0,1:T(4,128)}, u32[]{:S(2)}) copy-start(s32[16,4]{0,1:T(4,128)} %param.7) | copy-start | bytes 772
  23.4 112.0 %all-gather.8.cloned.1.call-start = ((), (), s32[]{:S(2)}) async-start(), calls=%async_computation.2 | async-start | bytes 6963200 | tf_op jit(solution)/shard_map/all_gather | solution.py:181
  24.3 151.1 %all-gather.6.cloned.1.call-start = ((), (), s32[]{:S(2)}) async-start(), calls=%async_computation.1 | async-start | bytes 4177920 | tf_op jit(solution)/shard_map/all_gather | solution.py:192
Sparse Core Ops, SparseCore 0:
  23.5 65.6 all-gather.3
  90.9 44.4 all-gather.7
  137.2 38.2 all-gather.5

commit v7 on v6

--- a/solution.py
+++ b/solution.py
@@ -13,7 +13,7 @@
 BLOCK_COLS = 512
 CHUNK_ROWS = 32
 SPLIT_BASE = 16
-SPLIT = (8, 13)
+SPLIT = (10,)
 COST_SCALE = 1000
 LOOKAHEAD = 2
 UNROLL = 8

time: 201 us -> 195 us (0.970)
  Pallas kernels: 84.2 us -> 81.5 us
    all_gather x1 -> x0, waiting for transfers between devices: 12.5 us -> none  [body(): gathered.append(lax.all_gather(piece, 'epoch', axis=0, tiled=True))]
    all_gather x2, waiting for transfers between devices: 71.4 us -> 81.9 us  [body(): lax.all_gather(pieces[i], 'epoch', axis=0, tiled=True)]
    pallas_call x3 -> x2, Pallas kernels: 84.2 us -> 81.5 us  [chunk_call(): pl.pallas_call(kernel, grid=(1,), out_shape=[jax.ShapeDtypeStruct((hyps,...]
  transfers between devices with their start and end apart: 5 -> 4, of which waited for: 5 -> 4; matrix products, arithmetic and copies ran while one was open for 1% -> 1% of each run, Pallas kernels for 32% -> 24%
where the time goes in v7:
time: 195 us
  waiting for transfers between devices  87.9 us (45%)
  Pallas kernels  81.5 us (42%)
  between operations  14.1 us (7%)
  starting transfers between devices  7.03 us (4%)
  other arithmetic  2.8 us (1%)
    all_gather x2, waiting for transfers between devices, body(): lax.all_gather(pieces[i], 'epoch', axis=0, tiled=True)  81.9 us
    pallas_call x2, Pallas kernels, chunk_call(): pl.pallas_call(kernel, grid=(1,), out_shape=[jax.ShapeDtypeStruct((hyps,...  81.5 us
    ppermute x1, starting transfers between devices, with_halo(): lax.ppermute(tail, axis, [(i, (i + 1) % count) for i in range(ends)])  5.66 us
    ppermute x1, waiting for transfers between devices, with_halo(): lax.ppermute(head, axis, [((i + 1) % count, i) for i in range(ends)])  5.08 us
  transfers between devices with their start and end apart: 4, of which 4 were waited for; matrix products, arithmetic and copies ran while one was open for 1% of the time, Pallas kernels for 24%

profile of v7, /device:TPU:1, one launch (start us, length us, event | category | flops | bytes accessed | tf_op | source)
XLA Modules:
  0.0 194.8 jit_solution(579771539996246907)
XLA Ops:
  7.2 0.0 copy-start
  7.2 0.0 copy-start.1
  7.2 0.0 all-gather.5.cloned.1.call-start
  7.2 1.0 pad_maximum_fusion.5
  8.3 5.7 %collective-permute-start = (bf16[1,2,8,4096]{3,2,1,0:T(8,128)(2,1)S(1)}, bf16[1,2,8,4096]{3,2,1,0:T(8,128)(2,1)S(1)}, u32[]{:S(2)}, u32[]{:S(2)}) collective-permute-start(bf16[1,2,8,4096]{3,2,1,0:T(8,128)(2,1)S(1)} %get-tuple-element.6), channel_id=1, source_target_pairs={{0,16},{16,32},{32,48},{48,64},{64,80},{80,96},{96,112},{1,17},{17... | collective-permute-start | bytes 393224 | tf_op jit(solution)/shard_map/ppermute | solution.py:30
  13.9 1.3 collective-permute-start.1
  15.2 0.8 collective-permute-done
  16.1 5.1 %collective-permute-done.1 = bf16[1,2,8,4096]{3,2,1,0:T(8,128)(2,1)S(1)} collective-permute-done((bf16[1,2,8,4096]{3,2,1,0:T(8,128)(2,1)S(1)}, bf16[1,2,8,4096]{3,2,1,0:T(8,128)(2,1)S(1)}, u32[]{:S(2)}, u32[]{:S(2)}) %collective-permute-start.1) | collective-permute-done | bytes 131104 | tf_op jit(solution)/shard_map/ppermute | solution.py:32
  21.1 0.0 copy-done
  21.1 0.0 copy-done.1
  21.1 0.9 pad_maximum_fusion
  22.1 0.0 copy-start.2
  22.1 0.0 copy-start.3
  22.1 0.0 all-gather.5.cloned.1.call-update
  22.1 0.0 all-gather.3.cloned.1.call-start
  22.2 0.8 pad_maximum_fusion.3
  23.0 0.0 all-gather.3.cloned.1.call-update
  23.0 0.0 copy-done.2
  23.0 0.1 copy.12
  23.1 0.7 reshape.10.rs_ref
  23.8 0.0 copy-done.3
  23.8 0.1 copy.13
  23.9 0.6 reshape.11.cs_ref
  24.5 75.8 %all-gather.5.cloned.1.call-done.mid_ref.left_ref = bf16[16,2,80,2560]{3,2,1,0:T(8,128)(2,1)} async-done(((bf16[1,2,80,2560]{3,2,1,0:T(8,128)(2,1)}), bf16[16,2,80,2560]{3,2,1,0:T(8,128)(2,1)}) %all-gather.5.cloned.1.call-update) | async-done | bytes 13107216 | tf_op jit(solution)/shard_map/all_gather | solution.py:181
  100.3 46.3 %shift_stack_0.1 = (f32[4,64,4096]{2,1,0:T(8,128)}, f32[4,64,4096]{2,1,0:T(8,128)}) custom-call(s32[64]{0:T(128)} %reshape.10.rs_ref, s32[64]{0:T(128)} %reshape.11.cs_ref, bf16[16,2,80,2560]{3,2,1,0:T(8,128)(2,1)} %all-gather.5.cloned.1.call-done.mid_ref.left_ref, bf16[16,2,80,2560]{3,2,1,0:T(8,128)(2,1)} %all-gather.5.cloned.1.call-done.mid_ref.left_ref), custom_call_target="tpu_custom_call" | custom-call | flops 39845888000 | bytes 19398656 | tf_op jit(solution)/shard_map/shift_stack_0/pallas_call | solution.py:143
  146.5 6.1 %all-gather.3.cloned.1.call-done.mid_ref = bf16[16,2,80,1536]{3,2,1,0:T(8,128)(2,1)} async-done(((bf16[1,2,80,1536]{3,2,1,0:T(8,128)(2,1)}), bf16[16,2,80,1536]{3,2,1,0:T(8,128)(2,1)}) %all-gather.3.cloned.1.call-update) | async-done | bytes 7864336 | tf_op jit(solution)/shard_map/all_gather | solution.py:181
  152.7 35.3 %shift_stack_1.1 = (f32[4,64,4096]{2,1,0:T(8,128)}, f32[4,64,4096]{2,1,0:T(8,128)}) custom-call(s32[64]{0:T(128)} %reshape.10.rs_ref, s32[64]{0:T(128)} %reshape.11.cs_ref, bf16[16,2,80,1536]{3,2,1,0:T(8,128)(2,1)} %all-gather.3.cloned.1.call-done.mid_ref, ...), custom_call_target="tpu_custom_call", output_to_operand_aliasing={{0}: (4, {}), {1}: (5, {})} | custom-call | flops 27262976000 | bytes 12582912 | tf_op jit(solution)/shard_map/shift_stack_1/pallas_call | solution.py:143
Async XLA Ops:
  7.2 14.0 %copy-start = (bf16[1,64,4096]{2,1,0:T(8,128)(2,1)S(1)}, bf16[1,64,4096]{2,1,0:T(8,128)(2,1)}, u32[]{:S(2)}) copy-start(bf16[1,64,4096]{2,1,0:T(8,128)(2,1)} %param.5) | copy-start | bytes 1572868
  7.2 14.0 %copy-start.1 = (bf16[1,64,4096]{2,1,0:T(8,128)(2,1)S(1)}, bf16[1,64,4096]{2,1,0:T(8,128)(2,1)}, u32[]{:S(2)}) copy-start(bf16[1,64,4096]{2,1,0:T(8,128)(2,1)} %param.4) | copy-start | bytes 1572868
  7.2 93.1 %all-gather.5.cloned.1.call-start = ((), (), s32[]{:S(2)}) async-start(), calls=%async_computation.1 | async-start | bytes 13926400 | tf_op jit(solution)/shard_map/all_gather | solution.py:181
  8.3 7.8 %collective-permute-start = (bf16[1,2,8,4096]{3,2,1,0:T(8,128)(2,1)S(1)}, bf16[1,2,8,4096]{3,2,1,0:T(8,128)(2,1)S(1)}, u32[]{:S(2)}, u32[]{:S(2)}) collective-permute-start(bf16[1,2,8,4096]{3,2,1,0:T(8,128)(2,1)S(1)} %get-tuple-element.6), channel_id=1, source_target_pairs={{0,16},{16,32},{32,48},{48,64},{64,80},{80,96},{96,112},{1,17},{17... | collective-permute-start | bytes 393224 | tf_op jit(solution)/shard_map/ppermute | solution.py:30
  13.9 7.2 %collective-permute-start.1 = (bf16[1,2,8,4096]{3,2,1,0:T(8,128)(2,1)S(1)}, bf16[1,2,8,4096]{3,2,1,0:T(8,128)(2,1)S(1)}, u32[]{:S(2)}, u32[]{:S(2)}) collective-permute-start(bf16[1,2,8,4096]{3,2,1,0:T(8,128)(2,1)S(1)} %get-tuple-element.7), channel_id=1, source_target_pairs={{16,0},{32,16},{48,32},{64,48},{80,64},{96,80},{112,96},{17,1},{33... | collective-permute-start | bytes 393224 | tf_op jit(solution)/shard_map/ppermute | solution.py:32
  22.1 0.9 copy-start.2
  22.1 1.7 copy-start.3
  22.1 130.6 %all-gather.3.cloned.1.call-start = ((), (), s32[]{:S(2)}) async-start(), calls=%async_computation | async-start | bytes 8355840 | tf_op jit(solution)/shard_map/all_gather | solution.py:181
Sparse Core Ops, SparseCore 0:
  22.2 77.9 all-gather.4
  102.0 50.6 all-gather.2

commit v8 on v7

--- a/solution.py
+++ b/solution.py
@@ -49,20 +49,18 @@
         pieces = min(BLOCK_COLS // LANES, (out_hi - at) // LANES)
         subs.append((at, pieces))
         at += pieces * LANES
-    copies = []
-    for img, out_hbm in ((0, psi_hbm), (1, phi_hbm)):
-        def convert(e, carry):
-            if first:
-                slab_ref[e, 0:rows_in, 0:side] = jnp.zeros((rows_in, side), jnp.float32)
-            else:
-                slab_ref[e, 0:rows_in, 0:side] = left_ref[e, img].astype(jnp.float32)
-            slab_ref[e, 0:rows_in, side:side + chunk] = mid_ref[e, img].astype(jnp.float32)
-            slab_ref[e, 0:rows_in, side + chunk:slab_cols] = jnp.zeros((rows_in, slab_cols - side - chunk), jnp.float32)
-            slab_ref[e, rows_in:slab_rows, :] = jnp.zeros((slab_rows - rows_in, slab_cols), jnp.float32)
-            return carry
-
-        lax.fori_loop(0, epochs, convert, 0)
-
+    img = pl.program_id(0)
+    e_now = pl.program_id(1)
+    if first:
+        slab_ref[e_now, 0:rows_in, 0:side] = jnp.zeros((rows_in, side), jnp.float32)
+    else:
+        slab_ref[e_now, 0:rows_in, 0:side] = left_ref[0, 0].astype(jnp.float32)
+    slab_ref[e_now, 0:rows_in, side:side + chunk] = mid_ref[0, 0].astype(jnp.float32)
+    slab_ref[e_now, 0:rows_in, side + chunk:slab_cols] = jnp.zeros((rows_in, slab_cols - side - chunk), jnp.float32)
+    slab_ref[e_now, rows_in:slab_rows, :] = jnp.zeros((slab_rows - rows_in, slab_cols), jnp.float32)
+
+    @pl.when(e_now == epochs - 1)
+    def _():
         def one_hyp(h, carry):
             for rchunk in range(rows_out // CHUNK_ROWS):
                 y0 = rchunk * CHUNK_ROWS
@@ -107,15 +105,16 @@
             return carry
 
         lax.fori_loop(0, hyps, one_hyp, 0)
-        copy = pltpu.make_async_copy(
-            out_vmem.at[img, :, :, pl.ds(0, width)],
-            out_hbm.at[:, :, pl.ds(col_base + out_lo, width)],
-            sems.at[img],
-        )
-        copy.start()
-        copies.append(copy)
-    for copy in copies:
-        copy.wait()
+        for index, out_hbm in enumerate((psi_hbm, phi_hbm)):
+            @pl.when(img == index)
+            def _():
+                copy = pltpu.make_async_copy(
+                    out_vmem.at[index, :, :, pl.ds(0, width)],
+                    out_hbm.at[:, :, pl.ds(col_base + out_lo, width)],
+                    sems.at[index],
+                )
+                copy.start()
+                copy.wait()
 
 
 def chunk_call(mid, prev, rs, cs, psi_acc, phi_acc, *, index, count, start, rows_out, hyps, cols):
@@ -142,13 +141,13 @@
     flops = 2 * epochs * hyps * images * rows_out * width * COST_SCALE
     return pl.pallas_call(
         kernel,
-        grid=(1,),
+        grid=(images, epochs),
         out_shape=[jax.ShapeDtypeStruct((hyps, rows_out, cols), jnp.float32)] * 2,
         in_specs=[
             pl.BlockSpec(memory_space=smem),
             pl.BlockSpec(memory_space=smem),
-            pl.BlockSpec((epochs, images, rows_in, chunk), lambda i: (0, 0, 0, 0)),
-            pl.BlockSpec((epochs, images, rows_in, side), lambda i: (0, 0, 0, prev_block)),
+            pl.BlockSpec((1, 1, rows_in, chunk), lambda i, e: (e, i, 0, 0)),
+            pl.BlockSpec((1, 1, rows_in, side), lambda i, e: (e, i, 0, prev_block)),
         ] + ([] if psi_acc is None else [pl.BlockSpec(memory_space=pl.ANY)] * 2),
         out_specs=[pl.BlockSpec(memory_space=pl.ANY), pl.BlockSpec(memory_space=pl.ANY)],
         scratch_shapes=[

time: 195 us -> 215 us (1.10)
  Pallas kernels: 81.5 us -> 107 us
  waiting for transfers between devices: 87.9 us -> 81.8 us
    pallas_call x2, Pallas kernels: 81.5 us -> 107 us  [chunk_call(): pl.pallas_call(kernel, grid=(images, epochs), out_shape=[jax.ShapeDtypeSt...]
    all_gather x2, waiting for transfers between devices: 81.9 us -> 75.8 us  [body(): lax.all_gather(pieces[i], 'epoch', axis=0, tiled=True)]
  transfers between devices with their start and end apart: 4 -> 4, of which waited for: 4 -> 3; matrix products, arithmetic and copies ran while one was open for 1% -> 1% of each run, Pallas kernels for 24% -> 27%
where the time goes in v8:
time: 215 us; the launch traced here: 214 us
  Pallas kernels  107 us (50%)
  waiting for transfers between devices  81.8 us (38%)
  between operations  14.1 us (7%)
  starting transfers between devices  7.03 us (3%)
  other arithmetic  2.8 us (1%)
    pallas_call x2, Pallas kernels, chunk_call(): pl.pallas_call(kernel, grid=(images, epochs), out_shape=[jax.ShapeDtypeSt...  107 us
    all_gather x2, waiting for transfers between devices, body(): lax.all_gather(pieces[i], 'epoch', axis=0, tiled=True)  75.8 us
    ppermute x1, starting transfers between devices, with_halo(): lax.ppermute(tail, axis, [(i, (i + 1) % count) for i in range(ends)])  5.66 us
    ppermute x1, waiting for transfers between devices, with_halo(): lax.ppermute(head, axis, [((i + 1) % count, i) for i in range(ends)])  5.08 us
  transfers between devices with their start and end apart: 4, of which 3 were waited for; matrix products, arithmetic and copies ran while one was open for 1% of the time, Pallas kernels for 27%

profile of v8, /device:TPU:1, one launch (start us, length us, event | category | flops | bytes accessed | tf_op | source)
XLA Modules:
  0.0 214.0 jit_solution(4329319807924562759)
XLA Ops:
  7.2 0.0 copy-start
  7.2 0.0 copy-start.1
  7.2 0.0 all-gather.5.cloned.1.call-start
  7.2 1.0 pad_maximum_fusion.5
  8.3 5.7 %collective-permute-start = (bf16[1,2,8,4096]{3,2,1,0:T(8,128)(2,1)S(1)}, bf16[1,2,8,4096]{3,2,1,0:T(8,128)(2,1)S(1)}, u32[]{:S(2)}, u32[]{:S(2)}) collective-permute-start(bf16[1,2,8,4096]{3,2,1,0:T(8,128)(2,1)S(1)} %get-tuple-element.6), channel_id=1, source_target_pairs={{0,16},{16,32},{32,48},{48,64},{64,80},{80,96},{96,112},{1,17},{17... | collective-permute-start | bytes 393224 | tf_op jit(solution)/shard_map/ppermute | solution.py:30
  13.9 1.3 collective-permute-start.1
  15.2 0.8 collective-permute-done
  16.1 5.1 %collective-permute-done.1 = bf16[1,2,8,4096]{3,2,1,0:T(8,128)(2,1)S(1)} collective-permute-done((bf16[1,2,8,4096]{3,2,1,0:T(8,128)(2,1)S(1)}, bf16[1,2,8,4096]{3,2,1,0:T(8,128)(2,1)S(1)}, u32[]{:S(2)}, u32[]{:S(2)}) %collective-permute-start.1) | collective-permute-done | bytes 131104 | tf_op jit(solution)/shard_map/ppermute | solution.py:32
  21.1 0.0 copy-done
  21.1 0.0 copy-done.1
  21.1 0.9 pad_maximum_fusion
  22.1 0.0 copy-start.2
  22.1 0.0 copy-start.3
  22.1 0.0 all-gather.5.cloned.1.call-update
  22.1 0.0 all-gather.3.cloned.1.call-start
  22.2 0.8 pad_maximum_fusion.3
  23.0 0.0 all-gather.3.cloned.1.call-update
  23.0 0.0 copy-done.2
  23.0 0.1 copy.12
  23.1 0.7 reshape.10.rs_ref
  23.8 0.0 copy-done.3
  23.8 0.1 copy.13
  23.9 0.6 reshape.11.cs_ref
  24.5 75.8 %all-gather.5.cloned.1.call-done.mid_ref.left_ref = bf16[16,2,80,2560]{3,2,1,0:T(8,128)(2,1)} async-done(((bf16[1,2,80,2560]{3,2,1,0:T(8,128)(2,1)}), bf16[16,2,80,2560]{3,2,1,0:T(8,128)(2,1)}) %all-gather.5.cloned.1.call-update) | async-done | bytes 13107216 | tf_op jit(solution)/shard_map/all_gather | solution.py:180
  100.3 58.6 %shift_stack_0.1 = (f32[4,64,4096]{2,1,0:T(8,128)}, f32[4,64,4096]{2,1,0:T(8,128)}) custom-call(s32[64]{0:T(128)} %reshape.10.rs_ref, s32[64]{0:T(128)} %reshape.11.cs_ref, bf16[16,2,80,2560]{3,2,1,0:T(8,128)(2,1)} %all-gather.5.cloned.1.call-done.mid_ref.left_ref, bf16[16,2,80,2560]{3,2,1,0:T(8,128)(2,1)} %all-gather.5.cloned.1.call-done.mid_ref.left_ref), custom_call_target="tpu_custom_call" | custom-call | flops 39845888000 | bytes 19398656 | tf_op jit(solution)/shard_map/shift_stack_0/pallas_call | solution.py:142
  158.9 0.0 all-gather.3.cloned.1.call-done.mid_ref
  158.9 48.2 %shift_stack_1.1 = (f32[4,64,4096]{2,1,0:T(8,128)}, f32[4,64,4096]{2,1,0:T(8,128)}) custom-call(s32[64]{0:T(128)} %reshape.10.rs_ref, s32[64]{0:T(128)} %reshape.11.cs_ref, bf16[16,2,80,1536]{3,2,1,0:T(8,128)(2,1)} %all-gather.3.cloned.1.call-done.mid_ref, ...), custom_call_target="tpu_custom_call", output_to_operand_aliasing={{0}: (4, {}), {1}: (5, {})} | custom-call | flops 27262976000 | bytes 12582912 | tf_op jit(solution)/shard_map/shift_stack_1/pallas_call | solution.py:142
Async XLA Ops:
  7.2 14.0 %copy-start = (bf16[1,64,4096]{2,1,0:T(8,128)(2,1)S(1)}, bf16[1,64,4096]{2,1,0:T(8,128)(2,1)}, u32[]{:S(2)}) copy-start(bf16[1,64,4096]{2,1,0:T(8,128)(2,1)} %param.5) | copy-start | bytes 1572868
  7.2 14.0 %copy-start.1 = (bf16[1,64,4096]{2,1,0:T(8,128)(2,1)S(1)}, bf16[1,64,4096]{2,1,0:T(8,128)(2,1)}, u32[]{:S(2)}) copy-start(bf16[1,64,4096]{2,1,0:T(8,128)(2,1)} %param.4) | copy-start | bytes 1572868
  7.2 93.1 %all-gather.5.cloned.1.call-start = ((), (), s32[]{:S(2)}) async-start(), calls=%async_computation.1 | async-start | bytes 13926400 | tf_op jit(solution)/shard_map/all_gather | solution.py:180
  8.3 7.8 %collective-permute-start = (bf16[1,2,8,4096]{3,2,1,0:T(8,128)(2,1)S(1)}, bf16[1,2,8,4096]{3,2,1,0:T(8,128)(2,1)S(1)}, u32[]{:S(2)}, u32[]{:S(2)}) collective-permute-start(bf16[1,2,8,4096]{3,2,1,0:T(8,128)(2,1)S(1)} %get-tuple-element.6), channel_id=1, source_target_pairs={{0,16},{16,32},{32,48},{48,64},{64,80},{80,96},{96,112},{1,17},{17... | collective-permute-start | bytes 393224 | tf_op jit(solution)/shard_map/ppermute | solution.py:30
  13.9 7.2 %collective-permute-start.1 = (bf16[1,2,8,4096]{3,2,1,0:T(8,128)(2,1)S(1)}, bf16[1,2,8,4096]{3,2,1,0:T(8,128)(2,1)S(1)}, u32[]{:S(2)}, u32[]{:S(2)}) collective-permute-start(bf16[1,2,8,4096]{3,2,1,0:T(8,128)(2,1)S(1)} %get-tuple-element.7), channel_id=1, source_target_pairs={{16,0},{32,16},{48,32},{64,48},{80,64},{96,80},{112,96},{17,1},{33... | collective-permute-start | bytes 393224 | tf_op jit(solution)/shard_map/ppermute | solution.py:32
  22.1 0.9 copy-start.2
  22.1 1.7 copy-start.3
  22.1 136.8 %all-gather.3.cloned.1.call-start = ((), (), s32[]{:S(2)}) async-start(), calls=%async_computation | async-start | bytes 8355840 | tf_op jit(solution)/shard_map/all_gather | solution.py:180
Sparse Core Ops, SparseCore 0:
  22.2 77.9 all-gather.4
  102.0 50.6 all-gather.2

commit v9 on v8

--- a/solution.py
+++ b/solution.py
@@ -50,17 +50,19 @@
         subs.append((at, pieces))
         at += pieces * LANES
     img = pl.program_id(0)
-    e_now = pl.program_id(1)
-    if first:
-        slab_ref[e_now, 0:rows_in, 0:side] = jnp.zeros((rows_in, side), jnp.float32)
-    else:
-        slab_ref[e_now, 0:rows_in, 0:side] = left_ref[0, 0].astype(jnp.float32)
-    slab_ref[e_now, 0:rows_in, side:side + chunk] = mid_ref[0, 0].astype(jnp.float32)
-    slab_ref[e_now, 0:rows_in, side + chunk:slab_cols] = jnp.zeros((rows_in, slab_cols - side - chunk), jnp.float32)
-    slab_ref[e_now, rows_in:slab_rows, :] = jnp.zeros((slab_rows - rows_in, slab_cols), jnp.float32)
-
-    @pl.when(e_now == epochs - 1)
-    def _():
+    if True:
+        def convert(e, carry):
+            if first:
+                slab_ref[e, 0:rows_in, 0:side] = jnp.zeros((rows_in, side), jnp.float32)
+            else:
+                slab_ref[e, 0:rows_in, 0:side] = left_ref[e, 0].astype(jnp.float32)
+            slab_ref[e, 0:rows_in, side:side + chunk] = mid_ref[e, 0].astype(jnp.float32)
+            slab_ref[e, 0:rows_in, side + chunk:slab_cols] = jnp.zeros((rows_in, slab_cols - side - chunk), jnp.float32)
+            slab_ref[e, rows_in:slab_rows, :] = jnp.zeros((slab_rows - rows_in, slab_cols), jnp.float32)
+            return carry
+
+        lax.fori_loop(0, epochs, convert, 0)
+
         def one_hyp(h, carry):
             for rchunk in range(rows_out // CHUNK_ROWS):
                 y0 = rchunk * CHUNK_ROWS
@@ -141,13 +143,13 @@
     flops = 2 * epochs * hyps * images * rows_out * width * COST_SCALE
     return pl.pallas_call(
         kernel,
-        grid=(images, epochs),
+        grid=(images,),
         out_shape=[jax.ShapeDtypeStruct((hyps, rows_out, cols), jnp.float32)] * 2,
         in_specs=[
             pl.BlockSpec(memory_space=smem),
             pl.BlockSpec(memory_space=smem),
-            pl.BlockSpec((1, 1, rows_in, chunk), lambda i, e: (e, i, 0, 0)),
-            pl.BlockSpec((1, 1, rows_in, side), lambda i, e: (e, i, 0, prev_block)),
+            pl.BlockSpec((epochs, 1, rows_in, chunk), lambda i: (0, i, 0, 0)),
+            pl.BlockSpec((epochs, 1, rows_in, side), lambda i: (0, i, 0, prev_block)),
         ] + ([] if psi_acc is None else [pl.BlockSpec(memory_space=pl.ANY)] * 2),
         out_specs=[pl.BlockSpec(memory_space=pl.ANY), pl.BlockSpec(memory_space=pl.ANY)],
         scratch_shapes=[

time: 215 us -> 195 us (0.907)
  Pallas kernels: 107 us -> 80.8 us
  waiting for transfers between devices: 81.8 us -> 88.5 us
    pallas_call x2, Pallas kernels: 107 us -> 80.8 us  [chunk_call(): pl.pallas_call(kernel, grid=(images,), out_shape=[jax.ShapeDtypeStruct((h...]
    all_gather x2, waiting for transfers between devices: 75.8 us -> 82.6 us  [body(): lax.all_gather(pieces[i], 'epoch', axis=0, tiled=True)]
  transfers between devices with their start and end apart: 4 -> 4, of which waited for: 3 -> 4; matrix products, arithmetic and copies ran while one was open for 1% -> 1% of each run, Pallas kernels for 27% -> 23%
where the time goes in v9:
time: 195 us
  waiting for transfers between devices  88.5 us (45%)
  Pallas kernels  80.8 us (41%)
  between operations  14.1 us (7%)
  starting transfers between devices  7.03 us (4%)
  other arithmetic  2.8 us (1%)
    all_gather x2, waiting for transfers between devices, body(): lax.all_gather(pieces[i], 'epoch', axis=0, tiled=True)  82.6 us
    pallas_call x2, Pallas kernels, chunk_call(): pl.pallas_call(kernel, grid=(images,), out_shape=[jax.ShapeDtypeStruct((h...  80.8 us
    ppermute x1, starting transfers between devices, with_halo(): lax.ppermute(tail, axis, [(i, (i + 1) % count) for i in range(ends)])  5.66 us
    ppermute x1, waiting for transfers between devices, with_halo(): lax.ppermute(head, axis, [((i + 1) % count, i) for i in range(ends)])  5.08 us
  transfers between devices with their start and end apart: 4, of which 4 were waited for; matrix products, arithmetic and copies ran while one was open for 1% of the time, Pallas kernels for 23%

profile of v9, /device:TPU:1, one launch (start us, length us, event | category | flops | bytes accessed | tf_op | source)
XLA Modules:
  0.0 194.8 jit_solution(8027760889711713977)
XLA Ops:
  7.2 0.0 copy-start
  7.2 0.0 copy-start.1
  7.2 0.0 all-gather.5.cloned.1.call-start
  7.2 1.0 pad_maximum_fusion.5
  8.3 5.7 %collective-permute-start = (bf16[1,2,8,4096]{3,2,1,0:T(8,128)(2,1)S(1)}, bf16[1,2,8,4096]{3,2,1,0:T(8,128)(2,1)S(1)}, u32[]{:S(2)}, u32[]{:S(2)}) collective-permute-start(bf16[1,2,8,4096]{3,2,1,0:T(8,128)(2,1)S(1)} %get-tuple-element.6), channel_id=1, source_target_pairs={{0,16},{16,32},{32,48},{48,64},{64,80},{80,96},{96,112},{1,17},{17... | collective-permute-start | bytes 393224 | tf_op jit(solution)/shard_map/ppermute | solution.py:30
  13.9 1.3 collective-permute-start.1
  15.2 0.8 collective-permute-done
  16.1 5.1 %collective-permute-done.1 = bf16[1,2,8,4096]{3,2,1,0:T(8,128)(2,1)S(1)} collective-permute-done((bf16[1,2,8,4096]{3,2,1,0:T(8,128)(2,1)S(1)}, bf16[1,2,8,4096]{3,2,1,0:T(8,128)(2,1)S(1)}, u32[]{:S(2)}, u32[]{:S(2)}) %collective-permute-start.1) | collective-permute-done | bytes 131104 | tf_op jit(solution)/shard_map/ppermute | solution.py:32
  21.1 0.0 copy-done
  21.1 0.0 copy-done.1
  21.1 0.9 pad_maximum_fusion
  22.1 0.0 copy-start.2
  22.1 0.0 copy-start.3
  22.1 0.0 all-gather.5.cloned.1.call-update
  22.1 0.0 all-gather.3.cloned.1.call-start
  22.2 0.8 pad_maximum_fusion.3
  23.0 0.0 all-gather.3.cloned.1.call-update
  23.0 0.0 copy-done.2
  23.0 0.1 copy.12
  23.1 0.7 reshape.10.rs_ref
  23.8 0.0 copy-done.3
  23.8 0.1 copy.13
  23.9 0.6 reshape.11.cs_ref
  24.5 75.8 %all-gather.5.cloned.1.call-done.mid_ref.left_ref = bf16[16,2,80,2560]{3,2,1,0:T(8,128)(2,1)} async-done(((bf16[1,2,80,2560]{3,2,1,0:T(8,128)(2,1)}), bf16[16,2,80,2560]{3,2,1,0:T(8,128)(2,1)}) %all-gather.5.cloned.1.call-update) | async-done | bytes 13107216 | tf_op jit(solution)/shard_map/all_gather | solution.py:182
  100.3 45.6 %shift_stack_0.1 = (f32[4,64,4096]{2,1,0:T(8,128)}, f32[4,64,4096]{2,1,0:T(8,128)}) custom-call(s32[64]{0:T(128)} %reshape.10.rs_ref, s32[64]{0:T(128)} %reshape.11.cs_ref, bf16[16,2,80,2560]{3,2,1,0:T(8,128)(2,1)} %all-gather.5.cloned.1.call-done.mid_ref.left_ref, bf16[16,2,80,2560]{3,2,1,0:T(8,128)(2,1)} %all-gather.5.cloned.1.call-done.mid_ref.left_ref), custom_call_target="tpu_custom_call" | custom-call | flops 39845888000 | bytes 19398656 | tf_op jit(solution)/shard_map/shift_stack_0/pallas_call | solution.py:144
  145.9 6.8 %all-gather.3.cloned.1.call-done.mid_ref = bf16[16,2,80,1536]{3,2,1,0:T(8,128)(2,1)} async-done(((bf16[1,2,80,1536]{3,2,1,0:T(8,128)(2,1)}), bf16[16,2,80,1536]{3,2,1,0:T(8,128)(2,1)}) %all-gather.3.cloned.1.call-update) | async-done | bytes 7864336 | tf_op jit(solution)/shard_map/all_gather | solution.py:182
  152.7 35.2 %shift_stack_1.1 = (f32[4,64,4096]{2,1,0:T(8,128)}, f32[4,64,4096]{2,1,0:T(8,128)}) custom-call(s32[64]{0:T(128)} %reshape.10.rs_ref, s32[64]{0:T(128)} %reshape.11.cs_ref, bf16[16,2,80,1536]{3,2,1,0:T(8,128)(2,1)} %all-gather.3.cloned.1.call-done.mid_ref, ...), custom_call_target="tpu_custom_call", output_to_operand_aliasing={{0}: (4, {}), {1}: (5, {})} | custom-call | flops 27262976000 | bytes 12582912 | tf_op jit(solution)/shard_map/shift_stack_1/pallas_call | solution.py:144
Async XLA Ops:
  7.2 14.0 %copy-start = (bf16[1,64,4096]{2,1,0:T(8,128)(2,1)S(1)}, bf16[1,64,4096]{2,1,0:T(8,128)(2,1)}, u32[]{:S(2)}) copy-start(bf16[1,64,4096]{2,1,0:T(8,128)(2,1)} %param.5) | copy-start | bytes 1572868
  7.2 14.0 %copy-start.1 = (bf16[1,64,4096]{2,1,0:T(8,128)(2,1)S(1)}, bf16[1,64,4096]{2,1,0:T(8,128)(2,1)}, u32[]{:S(2)}) copy-start(bf16[1,64,4096]{2,1,0:T(8,128)(2,1)} %param.4) | copy-start | bytes 1572868
  7.2 93.1 %all-gather.5.cloned.1.call-start = ((), (), s32[]{:S(2)}) async-start(), calls=%async_computation.1 | async-start | bytes 13926400 | tf_op jit(solution)/shard_map/all_gather | solution.py:182
  8.3 7.8 %collective-permute-start = (bf16[1,2,8,4096]{3,2,1,0:T(8,128)(2,1)S(1)}, bf16[1,2,8,4096]{3,2,1,0:T(8,128)(2,1)S(1)}, u32[]{:S(2)}, u32[]{:S(2)}) collective-permute-start(bf16[1,2,8,4096]{3,2,1,0:T(8,128)(2,1)S(1)} %get-tuple-element.6), channel_id=1, source_target_pairs={{0,16},{16,32},{32,48},{48,64},{64,80},{80,96},{96,112},{1,17},{17... | collective-permute-start | bytes 393224 | tf_op jit(solution)/shard_map/ppermute | solution.py:30
  13.9 7.2 %collective-permute-start.1 = (bf16[1,2,8,4096]{3,2,1,0:T(8,128)(2,1)S(1)}, bf16[1,2,8,4096]{3,2,1,0:T(8,128)(2,1)S(1)}, u32[]{:S(2)}, u32[]{:S(2)}) collective-permute-start(bf16[1,2,8,4096]{3,2,1,0:T(8,128)(2,1)S(1)} %get-tuple-element.7), channel_id=1, source_target_pairs={{16,0},{32,16},{48,32},{64,48},{80,64},{96,80},{112,96},{17,1},{33... | collective-permute-start | bytes 393224 | tf_op jit(solution)/shard_map/ppermute | solution.py:32
  22.1 0.9 copy-start.2
  22.1 1.7 copy-start.3
  22.1 130.6 %all-gather.3.cloned.1.call-start = ((), (), s32[]{:S(2)}) async-start(), calls=%async_computation | async-start | bytes 8355840 | tf_op jit(solution)/shard_map/all_gather | solution.py:182
Sparse Core Ops, SparseCore 0:
  22.2 77.9 all-gather.4
  102.0 50.6 all-gather.2

commit v10 on v9

--- a/solution.py
+++ b/solution.py
@@ -16,7 +16,7 @@
 SPLIT = (10,)
 COST_SCALE = 1000
 LOOKAHEAD = 2
-UNROLL = 8
+UNROLL = 16
 
 
 def with_halo(cells, sides, width):

time: 195 us -> 185 us (0.949)
  Pallas kernels: 80.8 us -> 59.2 us
  waiting for transfers between devices: 88.5 us -> 101 us
    pallas_call x2, Pallas kernels: 80.8 us -> 59.2 us  [chunk_call(): pl.pallas_call(kernel, grid=(images,), out_shape=[jax.ShapeDtypeStruct((h...]
    all_gather x2, waiting for transfers between devices: 82.6 us -> 94.6 us  [body(): lax.all_gather(pieces[i], 'epoch', axis=0, tiled=True)]
  transfers between devices with their start and end apart: 4 -> 4, of which waited for: 4 -> 4; matrix products, arithmetic and copies ran while one was open for 1% -> 1% of each run, Pallas kernels for 23% -> 18%
where the time goes in v10:
time: 185 us
  waiting for transfers between devices  101 us (55%)
  Pallas kernels  59.2 us (32%)
  between operations  14.1 us (8%)
  starting transfers between devices  7.03 us (4%)
  other arithmetic  2.8 us (2%)
    all_gather x2, waiting for transfers between devices, body(): lax.all_gather(pieces[i], 'epoch', axis=0, tiled=True)  94.6 us
    pallas_call x2, Pallas kernels, chunk_call(): pl.pallas_call(kernel, grid=(images,), out_shape=[jax.ShapeDtypeStruct((h...  59.2 us
    ppermute x1, starting transfers between devices, with_halo(): lax.ppermute(tail, axis, [(i, (i + 1) % count) for i in range(ends)])  5.66 us
    ppermute x1, waiting for transfers between devices, with_halo(): lax.ppermute(head, axis, [((i + 1) % count, i) for i in range(ends)])  5.08 us
  transfers between devices with their start and end apart: 4, of which 4 were waited for; matrix products, arithmetic and copies ran while one was open for 1% of the time, Pallas kernels for 18%

profile of v10, /device:TPU:1, one launch (start us, length us, event | category | flops | bytes accessed | tf_op | source)
XLA Modules:
  0.0 185.1 jit_solution(14444633833923318426)
XLA Ops:
  7.2 0.0 copy-start
  7.2 0.0 copy-start.1
  7.2 0.0 all-gather.5.cloned.1.call-start
  7.2 1.0 pad_maximum_fusion.5
  8.3 5.7 %collective-permute-start = (bf16[1,2,8,4096]{3,2,1,0:T(8,128)(2,1)S(1)}, bf16[1,2,8,4096]{3,2,1,0:T(8,128)(2,1)S(1)}, u32[]{:S(2)}, u32[]{:S(2)}) collective-permute-start(bf16[1,2,8,4096]{3,2,1,0:T(8,128)(2,1)S(1)} %get-tuple-element.6), channel_id=1, source_target_pairs={{0,16},{16,32},{32,48},{48,64},{64,80},{80,96},{96,112},{1,17},{17... | collective-permute-start | bytes 393224 | tf_op jit(solution)/shard_map/ppermute | solution.py:30
  13.9 1.3 collective-permute-start.1
  15.2 0.8 collective-permute-done
  16.1 5.1 %collective-permute-done.1 = bf16[1,2,8,4096]{3,2,1,0:T(8,128)(2,1)S(1)} collective-permute-done((bf16[1,2,8,4096]{3,2,1,0:T(8,128)(2,1)S(1)}, bf16[1,2,8,4096]{3,2,1,0:T(8,128)(2,1)S(1)}, u32[]{:S(2)}, u32[]{:S(2)}) %collective-permute-start.1) | collective-permute-done | bytes 131104 | tf_op jit(solution)/shard_map/ppermute | solution.py:32
  21.1 0.0 copy-done
  21.1 0.0 copy-done.1
  21.1 0.9 pad_maximum_fusion
  22.1 0.0 copy-start.2
  22.1 0.0 copy-start.3
  22.1 0.0 all-gather.5.cloned.1.call-update
  22.1 0.0 all-gather.3.cloned.1.call-start
  22.2 0.8 pad_maximum_fusion.3
  23.0 0.0 all-gather.3.cloned.1.call-update
  23.0 0.0 copy-done.2
  23.0 0.1 copy.12
  23.1 0.7 reshape.10.rs_ref
  23.8 0.0 copy-done.3
  23.8 0.1 copy.13
  23.9 0.6 reshape.11.cs_ref
  24.5 75.8 %all-gather.5.cloned.1.call-done.mid_ref.left_ref = bf16[16,2,80,2560]{3,2,1,0:T(8,128)(2,1)} async-done(((bf16[1,2,80,2560]{3,2,1,0:T(8,128)(2,1)}), bf16[16,2,80,2560]{3,2,1,0:T(8,128)(2,1)}) %all-gather.5.cloned.1.call-update) | async-done | bytes 13107216 | tf_op jit(solution)/shard_map/all_gather | solution.py:182
  100.3 33.6 %shift_stack_0.1 = (f32[4,64,4096]{2,1,0:T(8,128)}, f32[4,64,4096]{2,1,0:T(8,128)}) custom-call(s32[64]{0:T(128)} %reshape.10.rs_ref, s32[64]{0:T(128)} %reshape.11.cs_ref, bf16[16,2,80,2560]{3,2,1,0:T(8,128)(2,1)} %all-gather.5.cloned.1.call-done.mid_ref.left_ref, bf16[16,2,80,2560]{3,2,1,0:T(8,128)(2,1)} %all-gather.5.cloned.1.call-done.mid_ref.left_ref), custom_call_target="tpu_custom_call" | custom-call | flops 39845888000 | bytes 19398656 | tf_op jit(solution)/shard_map/shift_stack_0/pallas_call | solution.py:144
  133.9 18.8 %all-gather.3.cloned.1.call-done.mid_ref = bf16[16,2,80,1536]{3,2,1,0:T(8,128)(2,1)} async-done(((bf16[1,2,80,1536]{3,2,1,0:T(8,128)(2,1)}), bf16[16,2,80,1536]{3,2,1,0:T(8,128)(2,1)}) %all-gather.3.cloned.1.call-update) | async-done | bytes 7864336 | tf_op jit(solution)/shard_map/all_gather | solution.py:182
  152.7 25.6 %shift_stack_1.1 = (f32[4,64,4096]{2,1,0:T(8,128)}, f32[4,64,4096]{2,1,0:T(8,128)}) custom-call(s32[64]{0:T(128)} %reshape.10.rs_ref, s32[64]{0:T(128)} %reshape.11.cs_ref, bf16[16,2,80,1536]{3,2,1,0:T(8,128)(2,1)} %all-gather.3.cloned.1.call-done.mid_ref, ...), custom_call_target="tpu_custom_call", output_to_operand_aliasing={{0}: (4, {}), {1}: (5, {})} | custom-call | flops 27262976000 | bytes 12582912 | tf_op jit(solution)/shard_map/shift_stack_1/pallas_call | solution.py:144
Async XLA Ops:
  7.2 14.0 %copy-start = (bf16[1,64,4096]{2,1,0:T(8,128)(2,1)S(1)}, bf16[1,64,4096]{2,1,0:T(8,128)(2,1)}, u32[]{:S(2)}) copy-start(bf16[1,64,4096]{2,1,0:T(8,128)(2,1)} %param.5) | copy-start | bytes 1572868
  7.2 14.0 %copy-start.1 = (bf16[1,64,4096]{2,1,0:T(8,128)(2,1)S(1)}, bf16[1,64,4096]{2,1,0:T(8,128)(2,1)}, u32[]{:S(2)}) copy-start(bf16[1,64,4096]{2,1,0:T(8,128)(2,1)} %param.4) | copy-start | bytes 1572868
  7.2 93.1 %all-gather.5.cloned.1.call-start = ((), (), s32[]{:S(2)}) async-start(), calls=%async_computation.1 | async-start | bytes 13926400 | tf_op jit(solution)/shard_map/all_gather | solution.py:182
  8.3 7.8 %collective-permute-start = (bf16[1,2,8,4096]{3,2,1,0:T(8,128)(2,1)S(1)}, bf16[1,2,8,4096]{3,2,1,0:T(8,128)(2,1)S(1)}, u32[]{:S(2)}, u32[]{:S(2)}) collective-permute-start(bf16[1,2,8,4096]{3,2,1,0:T(8,128)(2,1)S(1)} %get-tuple-element.6), channel_id=1, source_target_pairs={{0,16},{16,32},{32,48},{48,64},{64,80},{80,96},{96,112},{1,17},{17... | collective-permute-start | bytes 393224 | tf_op jit(solution)/shard_map/ppermute | solution.py:30
  13.9 7.2 %collective-permute-start.1 = (bf16[1,2,8,4096]{3,2,1,0:T(8,128)(2,1)S(1)}, bf16[1,2,8,4096]{3,2,1,0:T(8,128)(2,1)S(1)}, u32[]{:S(2)}, u32[]{:S(2)}) collective-permute-start(bf16[1,2,8,4096]{3,2,1,0:T(8,128)(2,1)S(1)} %get-tuple-element.7), channel_id=1, source_target_pairs={{16,0},{32,16},{48,32},{64,48},{80,64},{96,80},{112,96},{17,1},{33... | collective-permute-start | bytes 393224 | tf_op jit(solution)/shard_map/ppermute | solution.py:32
  22.1 0.9 copy-start.2
  22.1 1.7 copy-start.3
  22.1 130.6 %all-gather.3.cloned.1.call-start = ((), (), s32[]{:S(2)}) async-start(), calls=%async_computation | async-start | bytes 8355840 | tf_op jit(solution)/shard_map/all_gather | solution.py:182
Sparse Core Ops, SparseCore 0:
  22.2 77.9 all-gather.4
  102.0 50.6 all-gather.2

commit v11 on v10

--- a/solution.py
+++ b/solution.py
@@ -13,7 +13,7 @@
 BLOCK_COLS = 512
 CHUNK_ROWS = 32
 SPLIT_BASE = 16
-SPLIT = (10,)
+SPLIT = (12,)
 COST_SCALE = 1000
 LOOKAHEAD = 2
 UNROLL = 16

time: 185 us -> 183 us (0.989)
  waiting for transfers between devices: 101 us -> 96.7 us
    all_gather x2, waiting for transfers between devices: 94.6 us -> 90.8 us  [body(): lax.all_gather(pieces[i], 'epoch', axis=0, tiled=True)]
  transfers between devices with their start and end apart: 4 -> 4, of which waited for: 4 -> 4; matrix products, arithmetic and copies ran while one was open for 1% -> 1% of each run, Pallas kernels for 18% -> 22%
where the time goes in v11:
time: 183 us
  waiting for transfers between devices  96.7 us (53%)
  Pallas kernels  59.3 us (32%)
  between operations  14.1 us (8%)
  starting transfers between devices  7.16 us (4%)
  other arithmetic  3.83 us (2%)
    all_gather x2, waiting for transfers between devices, body(): lax.all_gather(pieces[i], 'epoch', axis=0, tiled=True)  90.8 us
    pallas_call x2, Pallas kernels, chunk_call(): pl.pallas_call(kernel, grid=(images,), out_shape=[jax.ShapeDtypeStruct((h...  59.3 us
    ppermute x1, starting transfers between devices, with_halo(): lax.ppermute(tail, axis, [(i, (i + 1) % count) for i in range(ends)])  5.79 us
    ppermute x1, waiting for transfers between devices, with_halo(): lax.ppermute(head, axis, [((i + 1) % count, i) for i in range(ends)])  5.08 us
  transfers between devices with their start and end apart: 4, of which 4 were waited for; matrix products, arithmetic and copies ran while one was open for 1% of the time, Pallas kernels for 22%

profile of v11, /device:TPU:1, one launch (start us, length us, event | category | flops | bytes accessed | tf_op | source)
XLA Modules:
  0.0 182.5 jit_solution(11931137267635846077)
XLA Ops:
  7.2 0.0 all-gather.5.cloned.1.call-start
  7.2 1.0 pad_maximum_fusion.5
  8.2 0.0 copy-start
  8.2 0.0 copy-start.1
  8.2 5.8 %collective-permute-start = (bf16[1,2,8,4096]{3,2,1,0:T(8,128)(2,1)S(1)}, bf16[1,2,8,4096]{3,2,1,0:T(8,128)(2,1)S(1)}, u32[]{:S(2)}, u32[]{:S(2)}) collective-permute-start(bf16[1,2,8,4096]{3,2,1,0:T(8,128)(2,1)S(1)} %get-tuple-element.6), channel_id=1, source_target_pairs={{0,16},{16,32},{32,48},{48,64},{64,80},{80,96},{96,112},{1,17},{17... | collective-permute-start | bytes 393224 | tf_op jit(solution)/shard_map/ppermute | solution.py:30
  14.0 1.3 collective-permute-start.1
  15.3 0.8 collective-permute-done
  16.1 5.1 %collective-permute-done.1 = bf16[1,2,8,4096]{3,2,1,0:T(8,128)(2,1)S(1)} collective-permute-done((bf16[1,2,8,4096]{3,2,1,0:T(8,128)(2,1)S(1)}, bf16[1,2,8,4096]{3,2,1,0:T(8,128)(2,1)S(1)}, u32[]{:S(2)}, u32[]{:S(2)}) %collective-permute-start.1) | collective-permute-done | bytes 131104 | tf_op jit(solution)/shard_map/ppermute | solution.py:32
  21.2 2.1 %pad_maximum_fusion = bf16[1,2,80,3072]{3,2,1,0:T(8,128)(2,1)} fusion(bf16[1,2,8,4096]{3,2,1,0:T(8,128)(2,1)S(1)} %collective-permute-done.1, bf16[1,2,8,4096]{3,2,1,0:T(8,128)(2,1)S(1)} %collective-permute-done, bf16[1,1,64,4096]{3,2,1,0:T(8,128)(2,1)} %bitcast.3, bf16[1,1,64,4096]{3,2,1,0:T(8,128)(2,1)} %bitcast.6), kind=kLoop, calls=%fused_computation | loop fusion | flops 3932160 | bytes 2293760 | tf_op jit(solution)/shard_map/concatenate | solution.py:28
  23.3 0.0 copy-start.2
  23.3 0.0 copy-start.3
  23.3 0.0 all-gather.5.cloned.1.call-update
  23.4 0.0 all-gather.3.cloned.1.call-start
  23.4 0.0 copy-done
  23.4 0.0 copy-done.1
  23.4 0.7 pad_maximum_fusion.3
  24.2 0.0 all-gather.3.cloned.1.call-update
  24.2 0.0 copy-done.2
  24.2 0.1 copy.12
  24.3 0.6 reshape.10.rs_ref
  24.9 0.0 copy-done.3
  24.9 0.1 copy.13
  25.0 0.7 reshape.11.cs_ref
  25.6 88.2 %all-gather.5.cloned.1.call-done.mid_ref.left_ref = bf16[16,2,80,3072]{3,2,1,0:T(8,128)(2,1)} async-done(((bf16[1,2,80,3072]{3,2,1,0:T(8,128)(2,1)}), bf16[16,2,80,3072]{3,2,1,0:T(8,128)(2,1)}) %all-gather.5.cloned.1.call-update) | async-done | bytes 15728656 | tf_op jit(solution)/shard_map/all_gather | solution.py:182
  113.9 39.7 %shift_stack_0.1 = (f32[4,64,4096]{2,1,0:T(8,128)}, f32[4,64,4096]{2,1,0:T(8,128)}) custom-call(s32[64]{0:T(128)} %reshape.10.rs_ref, s32[64]{0:T(128)} %reshape.11.cs_ref, bf16[16,2,80,3072]{3,2,1,0:T(8,128)(2,1)} %all-gather.5.cloned.1.call-done.mid_ref.left_ref, bf16[16,2,80,3072]{3,2,1,0:T(8,128)(2,1)} %all-gather.5.cloned.1.call-done.mid_ref.left_ref), custom_call_target="tpu_custom_call" | custom-call | flops 48234496000 | bytes 23068672 | tf_op jit(solution)/shard_map/shift_stack_0/pallas_call | solution.py:144
  153.6 2.5 %all-gather.3.cloned.1.call-done.mid_ref = bf16[16,2,80,1024]{3,2,1,0:T(8,128)(2,1)} async-done(((bf16[1,2,80,1024]{3,2,1,0:T(8,128)(2,1)}), bf16[16,2,80,1024]{3,2,1,0:T(8,128)(2,1)}) %all-gather.3.cloned.1.call-update) | async-done | bytes 5242896 | tf_op jit(solution)/shard_map/all_gather | solution.py:182
  156.1 19.5 %shift_stack_1.1 = (f32[4,64,4096]{2,1,0:T(8,128)}, f32[4,64,4096]{2,1,0:T(8,128)}) custom-call(s32[64]{0:T(128)} %reshape.10.rs_ref, s32[64]{0:T(128)} %reshape.11.cs_ref, bf16[16,2,80,1024]{3,2,1,0:T(8,128)(2,1)} %all-gather.3.cloned.1.call-done.mid_ref, ...), custom_call_target="tpu_custom_call", output_to_operand_aliasing={{0}: (4, {}), {1}: (5, {})} | custom-call | flops 18874368000 | bytes 8912896 | tf_op jit(solution)/shard_map/shift_stack_1/pallas_call | solution.py:144
Async XLA Ops:
  7.2 106.7 %all-gather.5.cloned.1.call-start = ((), (), s32[]{:S(2)}) async-start(), calls=%async_computation.1 | async-start | bytes 16711680 | tf_op jit(solution)/shard_map/all_gather | solution.py:182
  8.2 15.2 %copy-start = (bf16[1,64,4096]{2,1,0:T(8,128)(2,1)S(1)}, bf16[1,64,4096]{2,1,0:T(8,128)(2,1)}, u32[]{:S(2)}) copy-start(bf16[1,64,4096]{2,1,0:T(8,128)(2,1)} %param.5) | copy-start | bytes 1572868
  8.2 15.2 %copy-start.1 = (bf16[1,64,4096]{2,1,0:T(8,128)(2,1)S(1)}, bf16[1,64,4096]{2,1,0:T(8,128)(2,1)}, u32[]{:S(2)}) copy-start(bf16[1,64,4096]{2,1,0:T(8,128)(2,1)} %param.4) | copy-start | bytes 1572868
  8.2 7.9 %collective-permute-start = (bf16[1,2,8,4096]{3,2,1,0:T(8,128)(2,1)S(1)}, bf16[1,2,8,4096]{3,2,1,0:T(8,128)(2,1)S(1)}, u32[]{:S(2)}, u32[]{:S(2)}) collective-permute-start(bf16[1,2,8,4096]{3,2,1,0:T(8,128)(2,1)S(1)} %get-tuple-element.6), channel_id=1, source_target_pairs={{0,16},{16,32},{32,48},{48,64},{64,80},{80,96},{96,112},{1,17},{17... | collective-permute-start | bytes 393224 | tf_op jit(solution)/shard_map/ppermute | solution.py:30
  14.0 7.2 %collective-permute-start.1 = (bf16[1,2,8,4096]{3,2,1,0:T(8,128)(2,1)S(1)}, bf16[1,2,8,4096]{3,2,1,0:T(8,128)(2,1)S(1)}, u32[]{:S(2)}, u32[]{:S(2)}) collective-permute-start(bf16[1,2,8,4096]{3,2,1,0:T(8,128)(2,1)S(1)} %get-tuple-element.7), channel_id=1, source_target_pairs={{16,0},{32,16},{48,32},{64,48},{80,64},{96,80},{112,96},{17,1},{33... | collective-permute-start | bytes 393224 | tf_op jit(solution)/shard_map/ppermute | solution.py:32
  23.3 0.9 copy-start.2
  23.3 1.6 copy-start.3
  23.4 132.8 %all-gather.3.cloned.1.call-start = ((), (), s32[]{:S(2)}) async-start(), calls=%async_computation | async-start | bytes 5570560 | tf_op jit(solution)/shard_map/all_gather | solution.py:182
Sparse Core Ops, SparseCore 0:
  23.5 90.3 all-gather.4
  115.6 40.5 all-gather.2

commit v12 on v11

--- a/solution.py
+++ b/solution.py
@@ -10,7 +10,7 @@
 DEPTH = 8
 XMAX = 64
 LANES = 128
-BLOCK_COLS = 512
+BLOCK_COLS = 640
 CHUNK_ROWS = 32
 SPLIT_BASE = 16
 SPLIT = (12,)

time: 183 us -> 180 us (0.984)
  Pallas kernels: 59.3 us -> 53.2 us
  waiting for transfers between devices: 96.7 us -> 99.5 us
    pallas_call x2, Pallas kernels: 59.3 us -> 53.2 us  [chunk_call(): pl.pallas_call(kernel, grid=(images,), out_shape=[jax.ShapeDtypeStruct((h...]
    all_gather x2, waiting for transfers between devices: 90.8 us -> 93.5 us  [body(): lax.all_gather(pieces[i], 'epoch', axis=0, tiled=True)]
  transfers between devices with their start and end apart: 4 -> 4, of which waited for: 4 -> 4; matrix products, arithmetic and copies ran while one was open for 1% -> 1% of each run, Pallas kernels for 22% -> 21%
where the time goes in v12:
time: 180 us; the launch traced here: 179 us
  waiting for transfers between devices  99.5 us (55%)
  Pallas kernels  53.2 us (30%)
  between operations  14.1 us (8%)
  starting transfers between devices  7.16 us (4%)
  other arithmetic  3.83 us (2%)
    all_gather x2, waiting for transfers between devices, body(): lax.all_gather(pieces[i], 'epoch', axis=0, tiled=True)  93.5 us
    pallas_call x2, Pallas kernels, chunk_call(): pl.pallas_call(kernel, grid=(images,), out_shape=[jax.ShapeDtypeStruct((h...  53.2 us
    ppermute x1, starting transfers between devices, with_halo(): lax.ppermute(tail, axis, [(i, (i + 1) % count) for i in range(ends)])  5.79 us
    ppermute x1, waiting for transfers between devices, with_halo(): lax.ppermute(head, axis, [((i + 1) % count, i) for i in range(ends)])  5.08 us
  transfers between devices with their start and end apart: 4, of which 4 were waited for; matrix products, arithmetic and copies ran while one was open for 1% of the time, Pallas kernels for 21%

profile of v12, /device:TPU:1, one launch (start us, length us, event | category | flops | bytes accessed | tf_op | source)
XLA Modules:
  0.0 179.3 jit_solution(10375499170885033982)
XLA Ops:
  7.2 0.0 all-gather.5.cloned.1.call-start
  7.2 1.0 pad_maximum_fusion.5
  8.2 0.0 copy-start
  8.2 0.0 copy-start.1
  8.2 5.8 %collective-permute-start = (bf16[1,2,8,4096]{3,2,1,0:T(8,128)(2,1)S(1)}, bf16[1,2,8,4096]{3,2,1,0:T(8,128)(2,1)S(1)}, u32[]{:S(2)}, u32[]{:S(2)}) collective-permute-start(bf16[1,2,8,4096]{3,2,1,0:T(8,128)(2,1)S(1)} %get-tuple-element.6), channel_id=1, source_target_pairs={{0,16},{16,32},{32,48},{48,64},{64,80},{80,96},{96,112},{1,17},{17... | collective-permute-start | bytes 393224 | tf_op jit(solution)/shard_map/ppermute | solution.py:30
  14.0 1.3 collective-permute-start.1
  15.3 0.8 collective-permute-done
  16.1 5.1 %collective-permute-done.1 = bf16[1,2,8,4096]{3,2,1,0:T(8,128)(2,1)S(1)} collective-permute-done((bf16[1,2,8,4096]{3,2,1,0:T(8,128)(2,1)S(1)}, bf16[1,2,8,4096]{3,2,1,0:T(8,128)(2,1)S(1)}, u32[]{:S(2)}, u32[]{:S(2)}) %collective-permute-start.1) | collective-permute-done | bytes 131104 | tf_op jit(solution)/shard_map/ppermute | solution.py:32
  21.2 2.1 %pad_maximum_fusion = bf16[1,2,80,3072]{3,2,1,0:T(8,128)(2,1)} fusion(bf16[1,2,8,4096]{3,2,1,0:T(8,128)(2,1)S(1)} %collective-permute-done.1, bf16[1,2,8,4096]{3,2,1,0:T(8,128)(2,1)S(1)} %collective-permute-done, bf16[1,1,64,4096]{3,2,1,0:T(8,128)(2,1)} %bitcast.3, bf16[1,1,64,4096]{3,2,1,0:T(8,128)(2,1)} %bitcast.6), kind=kLoop, calls=%fused_computation | loop fusion | flops 3932160 | bytes 2293760 | tf_op jit(solution)/shard_map/concatenate | solution.py:28
  23.3 0.0 copy-start.2
  23.3 0.0 copy-start.3
  23.3 0.0 all-gather.5.cloned.1.call-update
  23.4 0.0 all-gather.3.cloned.1.call-start
  23.4 0.0 copy-done
  23.4 0.0 copy-done.1
  23.4 0.7 pad_maximum_fusion.3
  24.2 0.0 all-gather.3.cloned.1.call-update
  24.2 0.0 copy-done.2
  24.2 0.1 copy.12
  24.3 0.6 reshape.10.rs_ref
  24.9 0.0 copy-done.3
  24.9 0.1 copy.13
  25.0 0.7 reshape.11.cs_ref
  25.6 88.2 %all-gather.5.cloned.1.call-done.mid_ref.left_ref = bf16[16,2,80,3072]{3,2,1,0:T(8,128)(2,1)} async-done(((bf16[1,2,80,3072]{3,2,1,0:T(8,128)(2,1)}), bf16[16,2,80,3072]{3,2,1,0:T(8,128)(2,1)}) %all-gather.5.cloned.1.call-update) | async-done | bytes 15728656 | tf_op jit(solution)/shard_map/all_gather | solution.py:182
  113.9 37.2 %shift_stack_0.1 = (f32[4,64,4096]{2,1,0:T(8,128)}, f32[4,64,4096]{2,1,0:T(8,128)}) custom-call(s32[64]{0:T(128)} %reshape.10.rs_ref, s32[64]{0:T(128)} %reshape.11.cs_ref, bf16[16,2,80,3072]{3,2,1,0:T(8,128)(2,1)} %all-gather.5.cloned.1.call-done.mid_ref.left_ref, bf16[16,2,80,3072]{3,2,1,0:T(8,128)(2,1)} %all-gather.5.cloned.1.call-done.mid_ref.left_ref), custom_call_target="tpu_custom_call" | custom-call | flops 48234496000 | bytes 23068672 | tf_op jit(solution)/shard_map/shift_stack_0/pallas_call | solution.py:144
  151.0 5.3 %all-gather.3.cloned.1.call-done.mid_ref = bf16[16,2,80,1024]{3,2,1,0:T(8,128)(2,1)} async-done(((bf16[1,2,80,1024]{3,2,1,0:T(8,128)(2,1)}), bf16[16,2,80,1024]{3,2,1,0:T(8,128)(2,1)}) %all-gather.3.cloned.1.call-update) | async-done | bytes 5242896 | tf_op jit(solution)/shard_map/all_gather | solution.py:182
  156.3 16.1 %shift_stack_1.1 = (f32[4,64,4096]{2,1,0:T(8,128)}, f32[4,64,4096]{2,1,0:T(8,128)}) custom-call(s32[64]{0:T(128)} %reshape.10.rs_ref, s32[64]{0:T(128)} %reshape.11.cs_ref, bf16[16,2,80,1024]{3,2,1,0:T(8,128)(2,1)} %all-gather.3.cloned.1.call-done.mid_ref, ...), custom_call_target="tpu_custom_call", output_to_operand_aliasing={{0}: (4, {}), {1}: (5, {})} | custom-call | flops 18874368000 | bytes 8912896 | tf_op jit(solution)/shard_map/shift_stack_1/pallas_call | solution.py:144
Async XLA Ops:
  7.2 106.7 %all-gather.5.cloned.1.call-start = ((), (), s32[]{:S(2)}) async-start(), calls=%async_computation.1 | async-start | bytes 16711680 | tf_op jit(solution)/shard_map/all_gather | solution.py:182
  8.2 15.2 %copy-start = (bf16[1,64,4096]{2,1,0:T(8,128)(2,1)S(1)}, bf16[1,64,4096]{2,1,0:T(8,128)(2,1)}, u32[]{:S(2)}) copy-start(bf16[1,64,4096]{2,1,0:T(8,128)(2,1)} %param.5) | copy-start | bytes 1572868
  8.2 15.2 %copy-start.1 = (bf16[1,64,4096]{2,1,0:T(8,128)(2,1)S(1)}, bf16[1,64,4096]{2,1,0:T(8,128)(2,1)}, u32[]{:S(2)}) copy-start(bf16[1,64,4096]{2,1,0:T(8,128)(2,1)} %param.4) | copy-start | bytes 1572868
  8.2 7.9 %collective-permute-start = (bf16[1,2,8,4096]{3,2,1,0:T(8,128)(2,1)S(1)}, bf16[1,2,8,4096]{3,2,1,0:T(8,128)(2,1)S(1)}, u32[]{:S(2)}, u32[]{:S(2)}) collective-permute-start(bf16[1,2,8,4096]{3,2,1,0:T(8,128)(2,1)S(1)} %get-tuple-element.6), channel_id=1, source_target_pairs={{0,16},{16,32},{32,48},{48,64},{64,80},{80,96},{96,112},{1,17},{17... | collective-permute-start | bytes 393224 | tf_op jit(solution)/shard_map/ppermute | solution.py:30
  14.0 7.2 %collective-permute-start.1 = (bf16[1,2,8,4096]{3,2,1,0:T(8,128)(2,1)S(1)}, bf16[1,2,8,4096]{3,2,1,0:T(8,128)(2,1)S(1)}, u32[]{:S(2)}, u32[]{:S(2)}) collective-permute-start(bf16[1,2,8,4096]{3,2,1,0:T(8,128)(2,1)S(1)} %get-tuple-element.7), channel_id=1, source_target_pairs={{16,0},{32,16},{48,32},{64,48},{80,64},{96,80},{112,96},{17,1},{33... | collective-permute-start | bytes 393224 | tf_op jit(solution)/shard_map/ppermute | solution.py:32
  23.3 0.9 copy-start.2
  23.3 1.6 copy-start.3
  23.4 133.0 %all-gather.3.cloned.1.call-start = ((), (), s32[]{:S(2)}) async-start(), calls=%async_computation | async-start | bytes 5570560 | tf_op jit(solution)/shard_map/all_gather | solution.py:182
Sparse Core Ops, SparseCore 0:
  23.5 90.3 all-gather.4
  115.6 40.7 all-gather.2

commit v13 on v12

--- a/solution.py
+++ b/solution.py
@@ -10,7 +10,7 @@
 DEPTH = 8
 XMAX = 64
 LANES = 128
-BLOCK_COLS = 640
+BLOCK_COLS = 768
 CHUNK_ROWS = 32
 SPLIT_BASE = 16
 SPLIT = (12,)

time: 180 us -> 180 us (level)
  transfers between devices with their start and end apart: 4 -> 4, of which waited for: 4 -> 4; matrix products, arithmetic and copies ran while one was open for 1% -> 1% of each run, Pallas kernels for 21% -> 20%
where the time goes in v13:
time: 180 us
  waiting for transfers between devices  99.8 us (55%)
  Pallas kernels  53.2 us (30%)
  between operations  14.1 us (8%)
  starting transfers between devices  7.16 us (4%)
  other arithmetic  3.83 us (2%)
    all_gather x2, waiting for transfers between devices, body(): lax.all_gather(pieces[i], 'epoch', axis=0, tiled=True)  93.8 us
    pallas_call x2, Pallas kernels, chunk_call(): pl.pallas_call(kernel, grid=(images,), out_shape=[jax.ShapeDtypeStruct((h...  53.2 us
    ppermute x1, starting transfers between devices, with_halo(): lax.ppermute(tail, axis, [(i, (i + 1) % count) for i in range(ends)])  5.79 us
    ppermute x1, waiting for transfers between devices, with_halo(): lax.ppermute(head, axis, [((i + 1) % count, i) for i in range(ends)])  5.08 us
  transfers between devices with their start and end apart: 4, of which 4 were waited for; matrix products, arithmetic and copies ran while one was open for 1% of the time, Pallas kernels for 20%

profile of v13, /device:TPU:1, one launch (start us, length us, event | category | flops | bytes accessed | tf_op | source)
XLA Modules:
  0.0 179.6 jit_solution(5310839826145486347)
XLA Ops:
  7.2 0.0 all-gather.5.cloned.1.call-start
  7.2 1.0 pad_maximum_fusion.5
  8.2 0.0 copy-start
  8.2 0.0 copy-start.1
  8.2 5.8 %collective-permute-start = (bf16[1,2,8,4096]{3,2,1,0:T(8,128)(2,1)S(1)}, bf16[1,2,8,4096]{3,2,1,0:T(8,128)(2,1)S(1)}, u32[]{:S(2)}, u32[]{:S(2)}) collective-permute-start(bf16[1,2,8,4096]{3,2,1,0:T(8,128)(2,1)S(1)} %get-tuple-element.6), channel_id=1, source_target_pairs={{0,16},{16,32},{32,48},{48,64},{64,80},{80,96},{96,112},{1,17},{17... | collective-permute-start | bytes 393224 | tf_op jit(solution)/shard_map/ppermute | solution.py:30
  14.0 1.3 collective-permute-start.1
  15.3 0.8 collective-permute-done
  16.1 5.1 %collective-permute-done.1 = bf16[1,2,8,4096]{3,2,1,0:T(8,128)(2,1)S(1)} collective-permute-done((bf16[1,2,8,4096]{3,2,1,0:T(8,128)(2,1)S(1)}, bf16[1,2,8,4096]{3,2,1,0:T(8,128)(2,1)S(1)}, u32[]{:S(2)}, u32[]{:S(2)}) %collective-permute-start.1) | collective-permute-done | bytes 131104 | tf_op jit(solution)/shard_map/ppermute | solution.py:32
  21.2 2.1 %pad_maximum_fusion = bf16[1,2,80,3072]{3,2,1,0:T(8,128)(2,1)} fusion(bf16[1,2,8,4096]{3,2,1,0:T(8,128)(2,1)S(1)} %collective-permute-done.1, bf16[1,2,8,4096]{3,2,1,0:T(8,128)(2,1)S(1)} %collective-permute-done, bf16[1,1,64,4096]{3,2,1,0:T(8,128)(2,1)} %bitcast.3, bf16[1,1,64,4096]{3,2,1,0:T(8,128)(2,1)} %bitcast.6), kind=kLoop, calls=%fused_computation | loop fusion | flops 3932160 | bytes 2293760 | tf_op jit(solution)/shard_map/concatenate | solution.py:28
  23.3 0.0 copy-start.2
  23.3 0.0 copy-start.3
  23.3 0.0 all-gather.5.cloned.1.call-update
  23.4 0.0 all-gather.3.cloned.1.call-start
  23.4 0.0 copy-done
  23.4 0.0 copy-done.1
  23.4 0.7 pad_maximum_fusion.3
  24.2 0.0 all-gather.3.cloned.1.call-update
  24.2 0.0 copy-done.2
  24.2 0.1 copy.12
  24.3 0.6 reshape.10.rs_ref
  24.9 0.0 copy-done.3
  24.9 0.1 copy.13
  25.0 0.7 reshape.11.cs_ref
  25.6 88.2 %all-gather.5.cloned.1.call-done.mid_ref.left_ref = bf16[16,2,80,3072]{3,2,1,0:T(8,128)(2,1)} async-done(((bf16[1,2,80,3072]{3,2,1,0:T(8,128)(2,1)}), bf16[16,2,80,3072]{3,2,1,0:T(8,128)(2,1)}) %all-gather.5.cloned.1.call-update) | async-done | bytes 15728656 | tf_op jit(solution)/shard_map/all_gather | solution.py:182
  113.9 36.5 %shift_stack_0.1 = (f32[4,64,4096]{2,1,0:T(8,128)}, f32[4,64,4096]{2,1,0:T(8,128)}) custom-call(s32[64]{0:T(128)} %reshape.10.rs_ref, s32[64]{0:T(128)} %reshape.11.cs_ref, bf16[16,2,80,3072]{3,2,1,0:T(8,128)(2,1)} %all-gather.5.cloned.1.call-done.mid_ref.left_ref, bf16[16,2,80,3072]{3,2,1,0:T(8,128)(2,1)} %all-gather.5.cloned.1.call-done.mid_ref.left_ref), custom_call_target="tpu_custom_call" | custom-call | flops 48234496000 | bytes 23068672 | tf_op jit(solution)/shard_map/shift_stack_0/pallas_call | solution.py:144
  150.4 5.6 %all-gather.3.cloned.1.call-done.mid_ref = bf16[16,2,80,1024]{3,2,1,0:T(8,128)(2,1)} async-done(((bf16[1,2,80,1024]{3,2,1,0:T(8,128)(2,1)}), bf16[16,2,80,1024]{3,2,1,0:T(8,128)(2,1)}) %all-gather.3.cloned.1.call-update) | async-done | bytes 5242896 | tf_op jit(solution)/shard_map/all_gather | solution.py:182
  156.0 16.7 %shift_stack_1.1 = (f32[4,64,4096]{2,1,0:T(8,128)}, f32[4,64,4096]{2,1,0:T(8,128)}) custom-call(s32[64]{0:T(128)} %reshape.10.rs_ref, s32[64]{0:T(128)} %reshape.11.cs_ref, bf16[16,2,80,1024]{3,2,1,0:T(8,128)(2,1)} %all-gather.3.cloned.1.call-done.mid_ref, ...), custom_call_target="tpu_custom_call", output_to_operand_aliasing={{0}: (4, {}), {1}: (5, {})} | custom-call | flops 18874368000 | bytes 8912896 | tf_op jit(solution)/shard_map/shift_stack_1/pallas_call | solution.py:144
Async XLA Ops:
  7.2 106.7 %all-gather.5.cloned.1.call-start = ((), (), s32[]{:S(2)}) async-start(), calls=%async_computation.1 | async-start | bytes 16711680 | tf_op jit(solution)/shard_map/all_gather | solution.py:182
  8.2 15.2 %copy-start = (bf16[1,64,4096]{2,1,0:T(8,128)(2,1)S(1)}, bf16[1,64,4096]{2,1,0:T(8,128)(2,1)}, u32[]{:S(2)}) copy-start(bf16[1,64,4096]{2,1,0:T(8,128)(2,1)} %param.5) | copy-start | bytes 1572868
  8.2 15.2 %copy-start.1 = (bf16[1,64,4096]{2,1,0:T(8,128)(2,1)S(1)}, bf16[1,64,4096]{2,1,0:T(8,128)(2,1)}, u32[]{:S(2)}) copy-start(bf16[1,64,4096]{2,1,0:T(8,128)(2,1)} %param.4) | copy-start | bytes 1572868
  8.2 7.9 %collective-permute-start = (bf16[1,2,8,4096]{3,2,1,0:T(8,128)(2,1)S(1)}, bf16[1,2,8,4096]{3,2,1,0:T(8,128)(2,1)S(1)}, u32[]{:S(2)}, u32[]{:S(2)}) collective-permute-start(bf16[1,2,8,4096]{3,2,1,0:T(8,128)(2,1)S(1)} %get-tuple-element.6), channel_id=1, source_target_pairs={{0,16},{16,32},{32,48},{48,64},{64,80},{80,96},{96,112},{1,17},{17... | collective-permute-start | bytes 393224 | tf_op jit(solution)/shard_map/ppermute | solution.py:30
  14.0 7.2 %collective-permute-start.1 = (bf16[1,2,8,4096]{3,2,1,0:T(8,128)(2,1)S(1)}, bf16[1,2,8,4096]{3,2,1,0:T(8,128)(2,1)S(1)}, u32[]{:S(2)}, u32[]{:S(2)}) collective-permute-start(bf16[1,2,8,4096]{3,2,1,0:T(8,128)(2,1)S(1)} %get-tuple-element.7), channel_id=1, source_target_pairs={{16,0},{32,16},{48,32},{64,48},{80,64},{96,80},{112,96},{17,1},{33... | collective-permute-start | bytes 393224 | tf_op jit(solution)/shard_map/ppermute | solution.py:32
  23.3 0.9 copy-start.2
  23.3 1.6 copy-start.3
  23.4 132.7 %all-gather.3.cloned.1.call-start = ((), (), s32[]{:S(2)}) async-start(), calls=%async_computation | async-start | bytes 5570560 | tf_op jit(solution)/shard_map/all_gather | solution.py:182
Sparse Core Ops, SparseCore 0:
  23.5 90.3 all-gather.4
  115.6 40.4 all-gather.2
